TPU v7x, 1024 devices: a whole 8x8x8 slice. The times are simulated.
1024 devices in a mesh: grp: 16 (over z, y_lo), mem: 64 (over x, y_hi, core).
Axes of the slice: x: 8, y: 8 (y_hi: 4, y_lo: 2; y = y_hi * 2 + y_lo), z: 8, core: 2. Of those that a mesh axis runs over, the one named last changes fastest.
Arguments:
- act: bfloat16 [3, 524288, 768], P(None, ('grp', 'mem')), may hold values from -6 to 6
- cot: bfloat16 [3, 524288, 192], P(None, ('grp', 'mem')), may hold values from -0.032958984 to 0.032958984
- owner: int32 [16, 3], P('grp'), may hold values from 0 to 63, as said below
- a_inverse: bfloat16 [64, 768, 768], P('mem'), as said below
- g_inverse: bfloat16 [64, 192, 192], P('mem'), as said below
Outputs:
- preconditioned: bfloat16 [3, 192, 768], P(None, None, 'mem')
Inputs may be any that keep to these rules, and one draw needn't show every extreme that they name: Each row of owner names 3 different members. `a_inverse`: each held factor is a dense symmetric matrix: a diagonal between 0.5 and 2 plus symmetric off-diagonal entries of scale about 0.5 / sqrt(order); not necessarily definite. `g_inverse`: each held factor is a dense symmetric matrix: a diagonal between 0.5 and 2 plus symmetric off-diagonal entries of scale about 0.5 / sqrt(order); not necessarily definite.
All inputs are finite; a program needn't handle non-finite values.
Results may differ from a plain program's by a relative error of at most 0.0058.
Values may be sent and summed in bfloat16 or wider, within the bound.
No kernel may reach another device: no remote copies, remote signals or barrier semaphores. Data moves between devices by JAX's collectives and lax.ppermute only.
A program may use at most 32 MiB of HBM per device.

v0:
```python
import jax
import jax.numpy as jnp
from jax import lax
from jax.sharding import PartitionSpec as P


def spread(block, axis, holder):
    block = jnp.where(lax.axis_index(axis) == holder, block, jnp.zeros_like(block))
    return lax.psum(block, axis)


def shards(act, cot, owner, a_inverse, g_inverse):
    layers = act.shape[0]
    local = jnp.einsum("lrd,lrh->ldh", cot, act, preferred_element_type=jnp.float32)
    shard = lax.psum_scatter(local, "mem", scatter_dimension=2, tiled=True).astype(jnp.bfloat16)
    width = shard.shape[2]
    member = lax.axis_index("mem")
    summed = lax.all_gather(shard, "mem", axis=2, tiled=True)
    results = []
    for layer in range(layers):
        holder = owner[0, layer]
        a_full, g_full = (spread(a_inverse[0], "mem", holder), spread(g_inverse[0], "mem", holder))
        left = jnp.dot(g_full, summed[layer], preferred_element_type=jnp.float32).astype(
            jnp.bfloat16
        )
        mine = lax.dynamic_slice_in_dim(a_full, member * width, width, 1)
        results.append(jnp.dot(left, mine, preferred_element_type=jnp.float32))
    total = lax.psum(jnp.stack(results), "grp")
    return total.astype(jnp.bfloat16)


def solution(mesh):
    in_specs = (
        P(None, ("grp", "mem"), None),
        P(None, ("grp", "mem"), None),
        P("grp", None),
        P("mem", None, None),
        P("mem", None, None),
    )
    out_specs = P(None, None, "mem")
    return jax.shard_map(shards, mesh=mesh, in_specs=in_specs, out_specs=out_specs, check_vma=False)
```

profile of v0, /device:TPU:8, one launch (start us, length us, event | category | flops | bytes accessed | tf_op | source)
XLA Modules:
  0.0 678.3 jit_solution(9151132939631354921)
XLA Ops:
  6.5 0.0 copy-start
  6.5 0.0 all-reduce.5.cloned.1.call-start
  6.5 1.4 fusion.19
  9.8 0.0 copy-start.2
  9.8 3.2 select_bitcast_fusion.2
  13.1 0.0 copy-done.2
  13.1 0.7 select_bitcast_fusion.5
  13.8 0.0 all-reduce.5.cloned.1.call-update
  13.8 0.0 copy-done
  13.8 1.0 copy-done.1
  14.9 2.4 fusion.20
  17.2 1.3 dynamic-slice
  19.1 316.3 %all-reduce.6 = bf16[3,192,768]{1,2,0:T(8,128)(2,1)S(1)} all-reduce(f32[3,192,768]{1,2,0:T(8,128)} %fusion.20), channel_id=2, replica_groups=mesh['grp'=16,'mem'=64] {'mem'}, use_global_device_ids=true, to_apply=%region_1.2.clone | all-reduce | flops 442368 | bytes 2654208
  335.4 82.5 %all_gather.3 = bf16[3,192,768]{1,0,2:T(4,128)(2,1)S(1)} all-gather(bf16[3,192,12]{1,0,2:T(4,128)(2,1)S(1)} %copy.10), channel_id=1, replica_groups=mesh['grp'=16,'mem'=64] {'mem'}, dimensions={2}, use_global_device_ids=true | all-gather | bytes 898560 | tf_op jit(solution)/shard_map/all_gather | solution.py:18
  418.0 2.6 fusion.18
  420.6 2.8 copy.17
  423.4 2.9 copy.18
  426.3 0.5 copy.19
  426.8 173.0 %all-reduce.5.cloned.1.call-done = (bf16[192,192]{1,0:T(8,128)(2,1)}, bf16[768,768]{1,0:T(8,128)(2,1)}, bf16[192,192]{1,0:T(8,128)(2,1)}, bf16[768,768]{1,0:T(8,...) async-done(((bf16[192,192]{1,0:T(8,128)(2,1)}, bf16[768,768]{1,0:T(8,128)(2,1)}, bf16[192,192]{1,0:T(8,128)(2,1)}, bf16[768,768]{1,0:T(8,128)(2,1)}, ...) | async-done | bytes 3760144 | tf_op jit(solution)/shard_map/psum | solution.py:9
  599.7 1.6 fusion.5
  601.3 1.6 fusion.4
  602.9 0.0 copy-done.3
  602.9 1.4 fusion.3
  604.3 67.1 %psum.55 = bf16[3,192,12]{1,2,0:T(8,128)(2,1)} all-reduce(f32[3,192,12]{1,2,0:T(8,128)S(1)} %pad_maximum_fusion), channel_id=1, replica_groups=mesh['grp'=16,'mem'=64] {'grp'}, use_global_device_ids=true, to_apply=%region_7.8 | all-reduce | flops 6912 | bytes 41472 | tf_op jit(solution)/shard_map/psum | solution.py:28
  (5 shorter events, 0.1 us)
Async XLA Ops:
  6.5 7.3 %copy-start = (bf16[3,512,768]{2,1,0:T(8,128)(2,1)S(1)}, bf16[3,512,768]{2,1,0:T(8,128)(2,1)}, u32[]{:S(2)}) copy-start(bf16[3,512,768]{2,1,0:T(8,128)(2,1)} %param.5) | copy-start | bytes 7077892
  6.5 593.2 %all-reduce.5.cloned.1.call-start = ((), (), s32[]{:S(2)}) async-start(), calls=%async_computation | async-start | bytes 7667712 | tf_op jit(solution)/shard_map/psum | solution.py:9
  9.8 3.3 copy-start.2
  13.8 1.1 copy-start.1
  599.7 3.1 copy-start.3
Sparse Core Ops, SparseCore 0:
  13.9 585.7 all-reduce.4
where the time goes:
time: 679 us; the launch traced here: 678 us
  blocking collectives  466 us (69%)
  waiting for transfers between devices  173 us (25%)
  between operations  15.9 us (2%)
  local copies, waits for them, and re-layouts  12.5 us (2%)
  matrix products  6.92 us (1%)
    unnamed x1, blocking collectives  316 us
    psum x1, waiting for transfers between devices, spread(): return lax.psum(block, axis)  173 us
    all_gather x1, blocking collectives, shards(): summed = lax.all_gather(shard, 'mem', axis=2, tiled=True)  82.5 us
    psum x1, blocking collectives, shards(): total = lax.psum(jnp.stack(results), 'grp')  67.1 us
  transfers between devices with their start and end apart: 1, of which 1 were waited for; matrix products, arithmetic and copies ran while one was open for 2% of the time, Pallas kernels for 0%

commit v1 on v0

v1 whole, which is shorter than its diff:
```python
import jax
import jax.numpy as jnp
from jax import lax
from jax.sharding import PartitionSpec as P


def shards(act, cot, owner, a_inverse, g_inverse):
    layers, rows, hid = act.shape
    dim = cot.shape[2]
    members = lax.axis_size("mem")
    width = hid // members
    member = lax.axis_index("mem")
    blocks = act.reshape(layers, rows, members, width)
    local = jnp.einsum("lrd,lrmc->mldc", cot, blocks, preferred_element_type=jnp.float32)
    parts = lax.all_to_all(local, "mem", 0, 0, tiled=True)
    shard = jnp.sum(parts, axis=0).astype(jnp.bfloat16)
    slots = lax.broadcasted_iota(jnp.int32, (members, 1, 1), 0)
    outgoing = jnp.zeros((members, dim, width), jnp.bfloat16)
    for layer in range(layers):
        outgoing = jnp.where(slots == owner[0, layer], shard[layer][None], outgoing)
    gathered = lax.all_to_all(outgoing, "mem", 0, 0, tiled=True)
    grad = jnp.transpose(gathered, (1, 0, 2)).reshape(dim, hid)
    left = jnp.dot(g_inverse[0], grad, preferred_element_type=jnp.float32).astype(jnp.bfloat16)
    term = jnp.dot(left, a_inverse[0], preferred_element_type=jnp.float32)
    pieces = jnp.transpose(term.reshape(dim, members, width), (1, 0, 2))
    returned = lax.all_to_all(pieces, "mem", 0, 0, tiled=True)
    mine = jnp.stack([returned[owner[0, layer]] for layer in range(layers)])
    total = lax.psum(mine, "grp")
    return total.astype(jnp.bfloat16)


def solution(mesh):
    in_specs = (
        P(None, ("grp", "mem"), None),
        P(None, ("grp", "mem"), None),
        P("grp", None),
        P("mem", None, None),
        P("mem", None, None),
    )
    out_specs = P(None, None, "mem")
    return jax.shard_map(shards, mesh=mesh, in_specs=in_specs, out_specs=out_specs, check_vma=False)
```

time: 679 us -> 260 us (0.38)
  the two profiles are of different devices: /device:TPU:8 before, /device:TPU:4 now
where the time goes in v1:
time: 260 us; the launch traced here: 259 us
  waiting for transfers between devices  113 us (43%)
  blocking collectives  72.2 us (28%)
  starting transfers between devices  43.2 us (17%)
  local copies, waits for them, and re-layouts  12.5 us (5%)
  matrix products  6.83 us (3%)
  between operations  5.82 us (2%)
  other arithmetic  5.18 us (2%)
    psum x1, blocking collectives, shards(): total = lax.psum(mine, 'grp')  72.2 us
    all_to_all x1, waiting for transfers between devices, shards(): parts = lax.all_to_all(local, 'mem', 0, 0, tiled=True)  69.9 us
    all_to_all x1, waiting for transfers between devices, shards(): returned = lax.all_to_all(pieces, 'mem', 0, 0, tiled=True)  25.2 us
    all_to_all x1, starting transfers between devices, shards(): gathered = lax.all_to_all(outgoing, 'mem', 0, 0, tiled=True)  19.7 us
    all_to_all x1, starting transfers between devices, shards(): parts = lax.all_to_all(local, 'mem', 0, 0, tiled=True)  18.3 us
    all_to_all x1, waiting for transfers between devices, shards(): gathered = lax.all_to_all(outgoing, 'mem', 0, 0, tiled=True)  18.3 us
  transfers between devices with their start and end apart: 3, of which 3 were waited for; matrix products, arithmetic and copies ran while one was open for 2% of the time, Pallas kernels for 0%

profile of v1, /device:TPU:4, one launch (start us, length us, event | category | flops | bytes accessed | tf_op | source)
XLA Modules:
  0.0 259.1 jit_solution(14562848256163818638)
XLA Ops:
  0.0 2.9 %copy.14 = bf16[3,512,768]{1,2,0:T(8,128)(2,1)S(1)} copy(bf16[3,512,768]{2,1,0:T(8,128)(2,1)} %param.5) | data formatting | bytes 4718592 | tf_op args[0]
  2.9 2.3 reshape.23
  5.2 4.6 %fusion.2 = f32[64,3,192,12]{2,0,3,1:T(8,128)S(1)} fusion(bf16[3,512,64,12]{1,3,2,0:T(8,128)(2,1)} %reshape.23, bf16[3,512,192]{1,2,0:T(8,128)(2,1)S(1)} %copy-done), kind=kOutput, calls=%fused_computation.2 | convolution fusion | flops 452984832 | bytes 4718592 | tf_op jit(solution)/shard_map/lrd,lrmc->mldc/dot_general | solution.py:14
  9.8 3.1 %copy.16 = f32[64,3,192,12]{2,3,1,0:T(8,128)} copy(f32[64,3,192,12]{2,0,3,1:T(8,128)S(1)} %fusion.2) | data formatting | bytes 3538944 | tf_op jit(solution)/shard_map/lrd,lrmc->mldc/transpose | solution.py:14
  12.9 18.3 %all-to-all-start = ((f32[64,3,192,12]{2,3,1,0:T(8,128)}), f32[64,3,192,12]{2,3,1,0:T(8,128)}, u32[]{:S(2)}, u32[]{:S(2)}) async-start(f32[64,3,192,12]{2,3,1,0:T(8,128)} %copy.16), calls=%async_computation | async-start | bytes 6291456 | tf_op jit(solution)/shard_map/all_to_all | solution.py:15
  31.3 0.6 fusion.10
  31.9 0.6 iota_compare_fusion.2
  32.5 1.3 iota_compare_fusion
  33.8 0.0 copy-start.1
  33.8 69.9 %all-to-all-done = f32[64,3,192,12]{2,3,1,0:T(8,128)} async-done(((f32[64,3,192,12]{2,3,1,0:T(8,128)}), f32[64,3,192,12]{2,3,1,0:T(8,128)}, u32[]{:S(2)}, u32[]{:S(2)}) %all-to-all-start) | async-done | bytes 1769504 | tf_op jit(solution)/shard_map/all_to_all | solution.py:15
  103.7 2.2 reduce_sum.9
  105.9 1.1 select_select_fusion
  107.0 19.7 %all-to-all-start.1 = ((bf16[64,192,12]{1,2,0:T(8,128)(2,1)}), bf16[64,192,12]{1,2,0:T(8,128)(2,1)S(1)}, u32[]{:S(2)}, u32[]{:S(2)}) async-start(bf16[64,192,12]{1,2,0:T(8,128)(2,1)} %select_select_fusion), calls=%async_computation.1 | async-start | bytes 1048576 | tf_op jit(solution)/shard_map/all_to_all | solution.py:21
  126.7 0.6 copy.17
  127.4 0.0 copy-start.3
  127.4 1.3 dot_general.16
  128.7 18.3 %all-to-all-done.1 = bf16[64,192,12]{1,2,0:T(8,128)(2,1)S(1)} async-done(((bf16[64,192,12]{1,2,0:T(8,128)(2,1)}), bf16[64,192,12]{1,2,0:T(8,128)(2,1)S(1)}, u32[]{:S(2)}, u32[]{:S(2)}) %all-to-all-start.1) | async-done | bytes 294944 | tf_op jit(solution)/shard_map/all_to_all | solution.py:21
  146.9 0.2 reshape.24
  147.1 0.0 copy-done.3
  147.1 2.3 convolution_bitcast_fusion
  149.4 1.4 copy.19
  150.8 5.2 %all-to-all-start.2 = ((f32[64,192,12]{1,2,0:T(8,128)}), f32[64,192,12]{1,2,0:T(8,128)S(1)}, u32[]{:S(2)}, u32[]{:S(2)}) async-start(f32[64,192,12]{1,2,0:T(8,128)} %copy.19), calls=%async_computation.2 | async-start | bytes 2097152 | tf_op jit(solution)/shard_map/all_to_all | solution.py:26
  161.7 25.2 %all-to-all-done.2 = f32[64,192,12]{1,2,0:T(8,128)S(1)} async-done(((f32[64,192,12]{1,2,0:T(8,128)}), f32[64,192,12]{1,2,0:T(8,128)S(1)}, u32[]{:S(2)}, u32[]{:S(2)}) %all-to-all-start.2) | async-done | bytes 589856 | tf_op jit(solution)/shard_map/all_to_all | solution.py:26
  186.9 72.2 %psum.7 = bf16[3,192,12]{1,2,0:T(8,128)(2,1)} all-reduce(f32[3,192,12]{1,2,0:T(8,128)S(1)} %pad_maximum_fusion), channel_id=1, replica_groups=mesh['grp'=16,'mem'=64] {'grp'}, use_global_device_ids=true, to_apply=%region_1.2 | all-reduce | flops 6912 | bytes 41472 | tf_op jit(solution)/shard_map/psum | solution.py:28
  (8 shorter events, 0.0 us)
Async XLA Ops:
  0.0 5.2 %copy-start = (bf16[3,512,192]{1,2,0:T(8,128)(2,1)S(1)}, bf16[3,512,192]{1,2,0:T(8,128)(2,1)}, u32[]{:S(2)}) copy-start(bf16[3,512,192]{1,2,0:T(8,128)(2,1)} %param.6) | copy-start | bytes 1769476
  12.9 18.4 %copy-start.2 = (s32[1,3]{1,0:T(1,128)S(1)}, s32[1,3]{1,0:T(1,128)}, u32[]{:S(2)}) copy-start(s32[1,3]{1,0:T(1,128)} %param.7) | copy-start | bytes 40
  12.9 90.8 %all-to-all-start = ((f32[64,3,192,12]{2,3,1,0:T(8,128)}), f32[64,3,192,12]{2,3,1,0:T(8,128)}, u32[]{:S(2)}, u32[]{:S(2)}) async-start(f32[64,3,192,12]{2,3,1,0:T(8,128)} %copy.16), calls=%async_computation | async-start | bytes 6291456 | tf_op jit(solution)/shard_map/all_to_all | solution.py:15
  33.8 92.9 %copy-start.1 = (bf16[1,768,768]{2,1,0:T(8,128)(2,1)S(1)}, bf16[1,768,768]{2,1,0:T(8,128)(2,1)}, u32[]{:S(2)}) copy-start(bf16[1,768,768]{2,1,0:T(8,128)(2,1)} %param.8) | copy-start | bytes 3538948
  107.0 40.0 %all-to-all-start.1 = ((bf16[64,192,12]{1,2,0:T(8,128)(2,1)}), bf16[64,192,12]{1,2,0:T(8,128)(2,1)S(1)}, u32[]{:S(2)}, u32[]{:S(2)}) async-start(bf16[64,192,12]{1,2,0:T(8,128)(2,1)} %select_select_fusion), calls=%async_computation.1 | async-start | bytes 1048576 | tf_op jit(solution)/shard_map/all_to_all | solution.py:21
  127.4 19.8 %copy-start.3 = (bf16[1,192,192]{2,1,0:T(8,128)(2,1)S(1)}, bf16[1,192,192]{2,1,0:T(8,128)(2,1)}, u32[]{:S(2)}) copy-start(bf16[1,192,192]{2,1,0:T(8,128)(2,1)} %param.9) | copy-start | bytes 221188
  150.8 36.0 %all-to-all-start.2 = ((f32[64,192,12]{1,2,0:T(8,128)}), f32[64,192,12]{1,2,0:T(8,128)S(1)}, u32[]{:S(2)}, u32[]{:S(2)}) async-start(f32[64,192,12]{1,2,0:T(8,128)} %copy.19), calls=%async_computation.2 | async-start | bytes 2097152 | tf_op jit(solution)/shard_map/all_to_all | solution.py:26

commit v2 on v1

--- a/solution.py
+++ b/solution.py
@@ -12,8 +12,8 @@
     member = lax.axis_index("mem")
     blocks = act.reshape(layers, rows, members, width)
     local = jnp.einsum("lrd,lrmc->mldc", cot, blocks, preferred_element_type=jnp.float32)
-    parts = lax.all_to_all(local, "mem", 0, 0, tiled=True)
-    shard = jnp.sum(parts, axis=0).astype(jnp.bfloat16)
+    parts = lax.all_to_all(local.astype(jnp.bfloat16), "mem", 0, 0, tiled=True)
+    shard = jnp.sum(parts, axis=0, dtype=jnp.float32).astype(jnp.bfloat16)
     slots = lax.broadcasted_iota(jnp.int32, (members, 1, 1), 0)
     outgoing = jnp.zeros((members, dim, width), jnp.bfloat16)
     for layer in range(layers):
@@ -25,7 +25,13 @@
     pieces = jnp.transpose(term.reshape(dim, members, width), (1, 0, 2))
     returned = lax.all_to_all(pieces, "mem", 0, 0, tiled=True)
     mine = jnp.stack([returned[owner[0, layer]] for layer in range(layers)])
-    total = lax.psum(mine, "grp")
+    groups = lax.axis_size("grp")
+    total = mine
+    step = 1
+    while step < groups:
+        pairs = [(i, i ^ step) for i in range(groups)]
+        total = total + lax.ppermute(total, "grp", pairs)
+        step *= 2
     return total.astype(jnp.bfloat16)
 
 

time: 260 us -> 175 us (0.67)
  the two profiles are of different devices: /device:TPU:4 before, /device:TPU:20 now
where the time goes in v2:
time: 175 us; the launch traced here: 174 us
  waiting for transfers between devices  92.2 us (53%)
  starting transfers between devices  53.9 us (31%)
  local copies, waits for them, and re-layouts  11.3 us (6%)
  matrix products  6.81 us (4%)
  between operations  5.65 us (3%)
  other arithmetic  3.91 us (2%)
    all_to_all x1, waiting for transfers between devices, shards(): parts = lax.all_to_all(local.astype(jnp.bfloat16), 'mem', 0, 0, tiled=True)  39.4 us
    ppermute x4, starting transfers between devices, shards(): total = total + lax.ppermute(total, 'grp', pairs)  29.7 us
    all_to_all x1, waiting for transfers between devices, shards(): returned = lax.all_to_all(pieces, 'mem', 0, 0, tiled=True)  25.4 us
    all_to_all x1, waiting for transfers between devices, shards(): gathered = lax.all_to_all(outgoing, 'mem', 0, 0, tiled=True)  18.2 us
    all_to_all x1, starting transfers between devices, shards(): parts = lax.all_to_all(local.astype(jnp.bfloat16), 'mem', 0, 0, tiled=True)  12.8 us
    ppermute x4, waiting for transfers between devices, shards(): total = total + lax.ppermute(total, 'grp', pairs)  9.15 us
    all_to_all x1, starting transfers between devices, shards(): gathered = lax.all_to_all(outgoing, 'mem', 0, 0, tiled=True)  6.29 us
    all_to_all x1, starting transfers between devices, shards(): returned = lax.all_to_all(pieces, 'mem', 0, 0, tiled=True)  5.16 us
  transfers between devices with their start and end apart: 7, of which 7 were waited for; matrix products, arithmetic and copies ran while one was open for 3% of the time, Pallas kernels for 0%

profile of v2, /device:TPU:20, one launch (start us, length us, event | category | flops | bytes accessed | tf_op | source)
XLA Modules:
  0.0 173.9 jit_solution(15013466783601335159)
XLA Ops:
  0.0 2.9 %copy.14 = bf16[3,512,768]{1,2,0:T(8,128)(2,1)S(1)} copy(bf16[3,512,768]{2,1,0:T(8,128)(2,1)} %param.5) | data formatting | bytes 4718592 | tf_op args[0]
  2.9 2.3 %reshape.23 = bf16[3,512,64,12]{1,3,2,0:T(8,128)(2,1)} reshape(bf16[3,512,768]{1,2,0:T(8,128)(2,1)S(1)} %copy.14) | data formatting | bytes 4718592 | tf_op jit(solution)/shard_map/reshape | solution.py:13
  5.3 4.6 %fusion.5 = bf16[64,3,192,12]{2,0,3,1:T(8,128)(2,1)S(1)} fusion(bf16[3,512,64,12]{1,3,2,0:T(8,128)(2,1)} %reshape.23, bf16[3,512,192]{1,2,0:T(8,128)(2,1)S(1)} %copy-done), kind=kOutput, calls=%fused_computation.3 | convolution fusion | flops 453427200 | bytes 3833856 | tf_op jit(solution)/shard_map/lrd,lrmc->mldc/dot_general | solution.py:14
  9.8 1.9 %copy.16 = bf16[64,3,192,12]{2,3,1,0:T(8,128)(2,1)} copy(bf16[64,3,192,12]{2,0,3,1:T(8,128)(2,1)S(1)} %fusion.5) | data formatting | bytes 1769472 | tf_op jit(solution)/shard_map/convert_element_type | solution.py:15
  11.7 12.8 %all-to-all-start = ((bf16[64,3,192,12]{2,3,1,0:T(8,128)(2,1)}), bf16[64,3,192,12]{2,3,1,0:T(8,128)(2,1)S(1)}, u32[]{:S(2)}, u32[]{:S(2)}) async-start(bf16[64,3,192,12]{2,3,1,0:T(8,128)(2,1)} %copy.16), calls=%async_computation | async-start | bytes 3145728 | tf_op jit(solution)/shard_map/all_to_all | solution.py:15
  25.1 0.6 iota_compare_fusion.2
  25.7 1.2 iota_compare_fusion
  26.9 39.4 %all-to-all-done = bf16[64,3,192,12]{2,3,1,0:T(8,128)(2,1)S(1)} async-done(((bf16[64,3,192,12]{2,3,1,0:T(8,128)(2,1)}), bf16[64,3,192,12]{2,3,1,0:T(8,128)(2,1)S(1)}, u32[]{:S(2)}, u32[]{:S(2)}) %all-to-all-start) | async-done | bytes 884768 | tf_op jit(solution)/shard_map/all_to_all | solution.py:15
  66.7 1.1 select_select_fusion
  67.8 6.3 %all-to-all-start.1 = ((bf16[64,192,12]{1,2,0:T(8,128)(2,1)}), bf16[64,192,12]{1,2,0:T(8,128)(2,1)S(1)}, u32[]{:S(2)}, u32[]{:S(2)}) async-start(bf16[64,192,12]{1,2,0:T(8,128)(2,1)} %select_select_fusion), calls=%async_computation.1 | async-start | bytes 1048576 | tf_op jit(solution)/shard_map/all_to_all | solution.py:21
  74.7 1.3 dot_general.16
  76.1 18.2 %all-to-all-done.1 = bf16[64,192,12]{1,2,0:T(8,128)(2,1)S(1)} async-done(((bf16[64,192,12]{1,2,0:T(8,128)(2,1)}), bf16[64,192,12]{1,2,0:T(8,128)(2,1)S(1)}, u32[]{:S(2)}, u32[]{:S(2)}) %all-to-all-start.1) | async-done | bytes 294944 | tf_op jit(solution)/shard_map/all_to_all | solution.py:21
  94.5 2.3 %convolution_bitcast_fusion = f32[64,192,12]{1,0,2:T(8,128)S(1)} fusion(bf16[64,12,768]{2,1,0:T(8,128)(2,1)} %dot_general.16, bf16[192,768]{0,1:T(8,128)(2,1)S(1)} %reshape.24, bf16[1,192,192]{2,1,0:T(8,128)(2,1)S(1)} %copy-done.3), kind=kOutput, calls=%fused_computation.4 | convolution fusion | flops 283262976 | bytes 2138112 | tf_op jit(solution)/shard_map/dot_general | solution.py:24
  96.8 1.4 copy.19
  98.2 5.2 %all-to-all-start.2 = ((f32[64,192,12]{1,2,0:T(8,128)}), f32[64,192,12]{1,2,0:T(8,128)S(1)}, u32[]{:S(2)}, u32[]{:S(2)}) async-start(f32[64,192,12]{1,2,0:T(8,128)} %copy.19), calls=%async_computation.2 | async-start | bytes 2097152 | tf_op jit(solution)/shard_map/all_to_all | solution.py:26
  108.9 25.4 %all-to-all-done.2 = f32[64,192,12]{1,2,0:T(8,128)S(1)} async-done(((f32[64,192,12]{1,2,0:T(8,128)}), f32[64,192,12]{1,2,0:T(8,128)S(1)}, u32[]{:S(2)}, u32[]{:S(2)}) %all-to-all-start.2) | async-done | bytes 589856 | tf_op jit(solution)/shard_map/all_to_all | solution.py:26
  134.3 6.6 %collective-permute-start = (f32[3,192,12]{1,2,0:T(8,128)S(1)}, f32[3,192,12]{1,2,0:T(8,128)S(1)}, u32[]{:S(2)}, u32[]{:S(2)}) collective-permute-start(f32[3,192,12]{1,2,0:T(8,128)S(1)} %pad_maximum_fusion), channel_id=1, source_target_pairs={{0,64},{64,0},{128,192},{192,128},{256,320},{320,256},{384,448},{4... | collective-permute-start | bytes 82952 | tf_op jit(solution)/shard_map/ppermute | solution.py:33
  141.0 2.1 %collective-permute-done = f32[3,192,12]{1,2,0:T(8,128)S(1)} collective-permute-done((f32[3,192,12]{1,2,0:T(8,128)S(1)}, f32[3,192,12]{1,2,0:T(8,128)S(1)}, u32[]{:S(2)}, u32[]{:S(2)}) %collective-permute-start) | collective-permute-done | bytes 27680 | tf_op jit(solution)/shard_map/ppermute | solution.py:33
  143.0 3.6 %collective-permute-start.1 = (f32[3,192,12]{1,2,0:T(8,128)S(1)}, f32[3,192,12]{1,2,0:T(8,128)S(1)}, u32[]{:S(2)}, u32[]{:S(2)}) collective-permute-start(f32[3,192,12]{1,2,0:T(8,128)S(1)} %fusion.13), channel_id=1, source_target_pairs={{0,128},{64,192},{128,0},{192,64},{256,384},{320,448},{384,256},{4... | collective-permute-start | bytes 82952 | tf_op jit(solution)/shard_map/ppermute | solution.py:33
  146.7 2.4 %collective-permute-done.1 = f32[3,192,12]{1,2,0:T(8,128)S(1)} collective-permute-done((f32[3,192,12]{1,2,0:T(8,128)S(1)}, f32[3,192,12]{1,2,0:T(8,128)S(1)}, u32[]{:S(2)}, u32[]{:S(2)}) %collective-permute-start.1) | collective-permute-done | bytes 27680 | tf_op jit(solution)/shard_map/ppermute | solution.py:33
  149.0 7.6 %collective-permute-start.2 = (f32[3,192,12]{1,2,0:T(8,128)S(1)}, f32[3,192,12]{1,2,0:T(8,128)S(1)}, u32[]{:S(2)}, u32[]{:S(2)}) collective-permute-start(f32[3,192,12]{1,2,0:T(8,128)S(1)} %fusion.16), channel_id=1, source_target_pairs={{0,256},{64,320},{128,384},{192,448},{256,0},{320,64},{384,128},{4... | collective-permute-start | bytes 82952 | tf_op jit(solution)/shard_map/ppermute | solution.py:33
  156.6 2.1 %collective-permute-done.2 = f32[3,192,12]{1,2,0:T(8,128)S(1)} collective-permute-done((f32[3,192,12]{1,2,0:T(8,128)S(1)}, f32[3,192,12]{1,2,0:T(8,128)S(1)}, u32[]{:S(2)}, u32[]{:S(2)}) %collective-permute-start.2) | collective-permute-done | bytes 27680 | tf_op jit(solution)/shard_map/ppermute | solution.py:33
  158.7 11.9 %collective-permute-start.3 = (f32[3,192,12]{1,2,0:T(8,128)S(1)}, f32[3,192,12]{1,2,0:T(8,128)S(1)}, u32[]{:S(2)}, u32[]{:S(2)}) collective-permute-start(f32[3,192,12]{1,2,0:T(8,128)S(1)} %add.26), channel_id=1, source_target_pairs={{0,512},{64,576},{128,640},{192,704},{256,768},{320,832},{384,896}... | collective-permute-start | bytes 82952 | tf_op jit(solution)/shard_map/ppermute | solution.py:33
  170.6 2.7 %collective-permute-done.3 = f32[3,192,12]{1,2,0:T(8,128)S(1)} collective-permute-done((f32[3,192,12]{1,2,0:T(8,128)S(1)}, f32[3,192,12]{1,2,0:T(8,128)S(1)}, u32[]{:S(2)}, u32[]{:S(2)}) %collective-permute-start.3) | collective-permute-done | bytes 27680 | tf_op jit(solution)/shard_map/ppermute | solution.py:33
  (19 shorter events, 2.5 us)
Async XLA Ops:
  0.0 5.2 %copy-start = (bf16[3,512,192]{1,2,0:T(8,128)(2,1)S(1)}, bf16[3,512,192]{1,2,0:T(8,128)(2,1)}, u32[]{:S(2)}) copy-start(bf16[3,512,192]{1,2,0:T(8,128)(2,1)} %param.6) | copy-start | bytes 1769476
  11.7 12.8 %copy-start.2 = (s32[1,3]{1,0:T(1,128)S(1)}, s32[1,3]{1,0:T(1,128)}, u32[]{:S(2)}) copy-start(s32[1,3]{1,0:T(1,128)} %param.7) | copy-start | bytes 40
  11.7 54.6 %all-to-all-start = ((bf16[64,3,192,12]{2,3,1,0:T(8,128)(2,1)}), bf16[64,3,192,12]{2,3,1,0:T(8,128)(2,1)S(1)}, u32[]{:S(2)}, u32[]{:S(2)}) async-start(bf16[64,3,192,12]{2,3,1,0:T(8,128)(2,1)} %copy.16), calls=%async_computation | async-start | bytes 3145728 | tf_op jit(solution)/shard_map/all_to_all | solution.py:15
  26.9 47.1 %copy-start.1 = (bf16[1,768,768]{2,1,0:T(8,128)(2,1)S(1)}, bf16[1,768,768]{2,1,0:T(8,128)(2,1)}, u32[]{:S(2)}) copy-start(bf16[1,768,768]{2,1,0:T(8,128)(2,1)} %param.8) | copy-start | bytes 3538948
  67.8 26.5 %all-to-all-start.1 = ((bf16[64,192,12]{1,2,0:T(8,128)(2,1)}), bf16[64,192,12]{1,2,0:T(8,128)(2,1)S(1)}, u32[]{:S(2)}, u32[]{:S(2)}) async-start(bf16[64,192,12]{1,2,0:T(8,128)(2,1)} %select_select_fusion), calls=%async_computation.1 | async-start | bytes 1048576 | tf_op jit(solution)/shard_map/all_to_all | solution.py:21
  74.7 19.8 %copy-start.3 = (bf16[1,192,192]{2,1,0:T(8,128)(2,1)S(1)}, bf16[1,192,192]{2,1,0:T(8,128)(2,1)}, u32[]{:S(2)}) copy-start(bf16[1,192,192]{2,1,0:T(8,128)(2,1)} %param.9) | copy-start | bytes 221188
  98.2 36.1 %all-to-all-start.2 = ((f32[64,192,12]{1,2,0:T(8,128)}), f32[64,192,12]{1,2,0:T(8,128)S(1)}, u32[]{:S(2)}, u32[]{:S(2)}) async-start(f32[64,192,12]{1,2,0:T(8,128)} %copy.19), calls=%async_computation.2 | async-start | bytes 2097152 | tf_op jit(solution)/shard_map/all_to_all | solution.py:26
  134.3 8.7 %collective-permute-start = (f32[3,192,12]{1,2,0:T(8,128)S(1)}, f32[3,192,12]{1,2,0:T(8,128)S(1)}, u32[]{:S(2)}, u32[]{:S(2)}) collective-permute-start(f32[3,192,12]{1,2,0:T(8,128)S(1)} %pad_maximum_fusion), channel_id=1, source_target_pairs={{0,64},{64,0},{128,192},{192,128},{256,320},{320,256},{384,448},{4... | collective-permute-start | bytes 82952 | tf_op jit(solution)/shard_map/ppermute | solution.py:33
  143.0 6.0 %collective-permute-start.1 = (f32[3,192,12]{1,2,0:T(8,128)S(1)}, f32[3,192,12]{1,2,0:T(8,128)S(1)}, u32[]{:S(2)}, u32[]{:S(2)}) collective-permute-start(f32[3,192,12]{1,2,0:T(8,128)S(1)} %fusion.13), channel_id=1, source_target_pairs={{0,128},{64,192},{128,0},{192,64},{256,384},{320,448},{384,256},{4... | collective-permute-start | bytes 82952 | tf_op jit(solution)/shard_map/ppermute | solution.py:33
  149.0 9.7 %collective-permute-start.2 = (f32[3,192,12]{1,2,0:T(8,128)S(1)}, f32[3,192,12]{1,2,0:T(8,128)S(1)}, u32[]{:S(2)}, u32[]{:S(2)}) collective-permute-start(f32[3,192,12]{1,2,0:T(8,128)S(1)} %fusion.16), channel_id=1, source_target_pairs={{0,256},{64,320},{128,384},{192,448},{256,0},{320,64},{384,128},{4... | collective-permute-start | bytes 82952 | tf_op jit(solution)/shard_map/ppermute | solution.py:33
  158.7 14.5 %collective-permute-start.3 = (f32[3,192,12]{1,2,0:T(8,128)S(1)}, f32[3,192,12]{1,2,0:T(8,128)S(1)}, u32[]{:S(2)}, u32[]{:S(2)}) collective-permute-start(f32[3,192,12]{1,2,0:T(8,128)S(1)} %add.26), channel_id=1, source_target_pairs={{0,512},{64,576},{128,640},{192,704},{256,768},{320,832},{384,896}... | collective-permute-start | bytes 82952 | tf_op jit(solution)/shard_map/ppermute | solution.py:33

commit v3 on v2

v3 whole, which is shorter than its diff:
```python
import jax
import jax.numpy as jnp
from jax import lax
from jax.sharding import Mesh
from jax.sharding import PartitionSpec as P

MEM = ("x", "yh", "core")
CHIPS = ("x", "yh")


def shards(act, cot, owner, a_inverse, g_inverse):
    layers, rows, hid = act.shape
    dim = cot.shape[2]
    members = lax.axis_size(MEM)
    cores = lax.axis_size("core")
    width = hid // members
    member = lax.axis_index(MEM)
    core = lax.axis_index("core")
    blocks = act.reshape(layers, rows, members, width)
    local = jnp.einsum("lrd,lrmc->mldc", cot, blocks, preferred_element_type=jnp.float32)
    local = local.reshape(members // cores, cores, layers, dim, width)
    keep = jnp.where(core == 0, local[:, 0], local[:, 1])
    send = jnp.where(core == 0, local[:, 1], local[:, 0])
    pair = keep + lax.ppermute(send, "core", [(0, 1), (1, 0)])
    parts = lax.all_to_all(pair, CHIPS, 0, 0, tiled=True)
    shard = jnp.sum(parts, axis=0).astype(jnp.bfloat16)
    slots = lax.broadcasted_iota(jnp.int32, (members, 1, 1), 0)
    outgoing = jnp.zeros((members, dim, width), jnp.bfloat16)
    for layer in range(layers):
        outgoing = jnp.where(slots == owner[0, layer], shard[layer][None], outgoing)
    gathered = lax.all_to_all(outgoing, MEM, 0, 0, tiled=True)
    grad = jnp.transpose(gathered, (1, 0, 2)).reshape(dim, hid)
    left = jnp.dot(g_inverse[0], grad, preferred_element_type=jnp.float32).astype(jnp.bfloat16)
    term = jnp.dot(left, a_inverse[0], preferred_element_type=jnp.float32)
    pieces = jnp.transpose(term.reshape(dim, members, width), (1, 0, 2))
    returned = lax.all_to_all(pieces, MEM, 0, 0, tiled=True)
    mine = jnp.stack([returned[owner[0, layer]] for layer in range(layers)])
    groups = lax.axis_size("grp")
    total = mine
    step = 1
    while step < groups:
        pairs = [(i, i ^ step) for i in range(groups)]
        total = total + lax.ppermute(total, "grp", pairs)
        step *= 2
    return total.astype(jnp.bfloat16)


def solution(mesh):
    chips = mesh.shape["mem"] // 2
    sizes = (mesh.shape["grp"], chips // 4, 4, 2)
    fine = Mesh(mesh.devices.reshape(sizes), ("grp",) + MEM)
    in_specs = (
        P(None, ("grp",) + MEM, None),
        P(None, ("grp",) + MEM, None),
        P("grp", None),
        P(MEM, None, None),
        P(MEM, None, None),
    )
    out_specs = P(None, None, MEM)
    return jax.shard_map(shards, mesh=fine, in_specs=in_specs, out_specs=out_specs, check_vma=False)
```

time: 175 us -> 190 us (1.086)
  the two profiles are of different devices: /device:TPU:20 before, /device:TPU:4 now
where the time goes in v3:
time: 190 us; the launch traced here: 189 us
  waiting for transfers between devices  94.8 us (50%)
  starting transfers between devices  58.4 us (31%)
  local copies, waits for them, and re-layouts  18.6 us (10%)
  matrix products  6.83 us (4%)
  between operations  5.88 us (3%)
  other arithmetic  4.38 us (2%)
    all_to_all x1, waiting for transfers between devices, shards(): parts = lax.all_to_all(pair, CHIPS, 0, 0, tiled=True)  36.6 us
    all_to_all x1, waiting for transfers between devices, shards(): returned = lax.all_to_all(pieces, MEM, 0, 0, tiled=True)  25.2 us
    ppermute x4, starting transfers between devices, shards(): total = total + lax.ppermute(total, 'grp', pairs)  23.5 us
    all_to_all x1, waiting for transfers between devices, shards(): gathered = lax.all_to_all(outgoing, MEM, 0, 0, tiled=True)  18.2 us
    all_to_all x1, starting transfers between devices, shards(): parts = lax.all_to_all(pair, CHIPS, 0, 0, tiled=True)  17 us
    ppermute x4, waiting for transfers between devices, shards(): total = total + lax.ppermute(total, 'grp', pairs)  11.9 us
    all_to_all x1, starting transfers between devices, shards(): gathered = lax.all_to_all(outgoing, MEM, 0, 0, tiled=True)  10.9 us
    all_to_all x1, starting transfers between devices, shards(): returned = lax.all_to_all(pieces, MEM, 0, 0, tiled=True)  5.16 us
  transfers between devices with their start and end apart: 8, of which 8 were waited for; matrix products, arithmetic and copies ran while one was open for 2% of the time, Pallas kernels for 0%

profile of v3, /device:TPU:4, one launch (start us, length us, event | category | flops | bytes accessed | tf_op | source)
XLA Modules:
  0.0 188.9 jit_solution(3006627174288972551)
XLA Ops:
  0.0 2.9 %copy.29 = bf16[3,512,768]{1,2,0:T(8,128)(2,1)S(1)} copy(bf16[3,512,768]{2,1,0:T(8,128)(2,1)} %param.5) | data formatting | bytes 4718592 | tf_op args[0]
  2.9 2.3 %reshape.30 = bf16[3,512,64,12]{1,3,2,0:T(8,128)(2,1)} reshape(bf16[3,512,768]{1,2,0:T(8,128)(2,1)S(1)} %copy.29) | data formatting | bytes 4718592 | tf_op jit(solution)/shard_map/reshape | solution.py:19
  5.2 4.6 %fusion.2 = f32[64,3,192,12]{2,0,3,1:T(8,128)S(1)} fusion(bf16[3,512,64,12]{1,3,2,0:T(8,128)(2,1)} %reshape.30, bf16[3,512,192]{1,2,0:T(8,128)(2,1)S(1)} %copy-done), kind=kOutput, calls=%fused_computation.2 | convolution fusion | flops 452984832 | bytes 4718592 | tf_op jit(solution)/shard_map/lrd,lrmc->mldc/dot_general | solution.py:20
  9.8 2.5 %reshape.31 = f32[32,2,3,192,12]{3,1,0,4,2:T(2,128)} reshape(f32[64,3,192,12]{2,0,3,1:T(8,128)S(1)} %fusion.2) | data formatting | bytes 3538944 | tf_op jit(solution)/shard_map/reshape | solution.py:21
  12.3 4.8 %fusion.11 = (f32[32,1,3,192,12]{3,1,0,4,2:T(1,128)S(1)}, f32[32,1,3,192,12]{3,1,0,4,2:T(1,128)S(1)}) fusion(f32[32,2,3,192,12]{3,1,0,4,2:T(2,128)} %reshape.31), kind=kLoop, calls=%fused_computation.24 | loop fusion | bytes 3538944 | tf_op jit(solution)/shard_map/slice | solution.py:22
  17.3 1.9 %collective-permute-start = (f32[32,3,192,12]{2,0,3,1:T(8,128)S(1)}, f32[32,3,192,12]{2,0,3,1:T(8,128)S(1)}, u32[]{:S(2)}, u32[]{:S(2)}) collective-permute-start(f32[32,3,192,12]{2,0,3,1:T(8,128)S(1)} %select_bitcast_fusion), channel_id=1, source_target_pairs={{0,1},{1,0},{2,3},{3,2},{4,5},{5,4},{6,7},{7,6},{8,9},{9,8},{10,11... | collective-permute-start | bytes 2654216 | tf_op jit(solution)/shard_map/ppermute | solution.py:24
  19.3 2.8 %collective-permute-done = f32[32,3,192,12]{2,0,3,1:T(8,128)S(1)} collective-permute-done((f32[32,3,192,12]{2,0,3,1:T(8,128)S(1)}, f32[32,3,192,12]{2,0,3,1:T(8,128)S(1)}, u32[]{:S(2)}, u32[]{:S(2)}) %collective-permute-start) | collective-permute-done | bytes 884768 | tf_op jit(solution)/shard_map/ppermute | solution.py:24
  22.5 1.9 copy.33
  24.4 17.0 %all-to-all-start = ((f32[32,3,192,12]{2,3,1,0:T(8,128)}), f32[32,3,192,12]{2,3,1,0:T(8,128)S(1)}, u32[]{:S(2)}, u32[]{:S(2)}) async-start(f32[32,3,192,12]{2,3,1,0:T(8,128)} %copy.33), calls=%async_computation | async-start | bytes 3145728 | tf_op jit(solution)/shard_map/all_to_all | solution.py:25
  43.9 36.6 %all-to-all-done = f32[32,3,192,12]{2,3,1,0:T(8,128)S(1)} async-done(((f32[32,3,192,12]{2,3,1,0:T(8,128)}), f32[32,3,192,12]{2,3,1,0:T(8,128)S(1)}, u32[]{:S(2)}, u32[]{:S(2)}) %all-to-all-start) | async-done | bytes 884768 | tf_op jit(solution)/shard_map/all_to_all | solution.py:25
  81.7 10.9 %all-to-all-start.1 = ((bf16[64,192,12]{1,2,0:T(8,128)(2,1)}), bf16[64,192,12]{1,2,0:T(8,128)(2,1)S(1)}, u32[]{:S(2)}, u32[]{:S(2)}) async-start(bf16[64,192,12]{1,2,0:T(8,128)(2,1)} %select_select_fusion), calls=%async_computation.1 | async-start | bytes 1048576 | tf_op jit(solution)/shard_map/all_to_all | solution.py:31
  94.7 18.2 %all-to-all-done.1 = bf16[64,192,12]{1,2,0:T(8,128)(2,1)S(1)} async-done(((bf16[64,192,12]{1,2,0:T(8,128)(2,1)}), bf16[64,192,12]{1,2,0:T(8,128)(2,1)S(1)}, u32[]{:S(2)}, u32[]{:S(2)}) %all-to-all-start.1) | async-done | bytes 294944 | tf_op jit(solution)/shard_map/all_to_all | solution.py:31
  113.1 2.3 %convolution_bitcast_fusion = f32[64,192,12]{1,0,2:T(8,128)S(1)} fusion(bf16[64,12,768]{2,1,0:T(8,128)(2,1)} %dot_general.16, bf16[192,768]{0,1:T(8,128)(2,1)S(1)} %reshape.32, bf16[1,192,192]{2,1,0:T(8,128)(2,1)S(1)} %copy-done.3), kind=kOutput, calls=%fused_computation.3 | convolution fusion | flops 283262976 | bytes 2138112 | tf_op jit(solution)/shard_map/dot_general | solution.py:34
  115.4 1.5 copy.36
  116.8 5.2 %all-to-all-start.2 = ((f32[64,192,12]{1,2,0:T(8,128)}), f32[64,192,12]{1,2,0:T(8,128)S(1)}, u32[]{:S(2)}, u32[]{:S(2)}) async-start(f32[64,192,12]{1,2,0:T(8,128)} %copy.36), calls=%async_computation.2 | async-start | bytes 2097152 | tf_op jit(solution)/shard_map/all_to_all | solution.py:36
  127.7 25.2 %all-to-all-done.2 = f32[64,192,12]{1,2,0:T(8,128)S(1)} async-done(((f32[64,192,12]{1,2,0:T(8,128)}), f32[64,192,12]{1,2,0:T(8,128)S(1)}, u32[]{:S(2)}, u32[]{:S(2)}) %all-to-all-start.2) | async-done | bytes 589856 | tf_op jit(solution)/shard_map/all_to_all | solution.py:36
  152.9 1.9 %collective-permute-start.1 = (f32[3,192,12]{1,2,0:T(8,128)S(1)}, f32[3,192,12]{1,2,0:T(8,128)S(1)}, u32[]{:S(2)}, u32[]{:S(2)}) collective-permute-start(f32[3,192,12]{1,2,0:T(8,128)S(1)} %pad_maximum_fusion), channel_id=1, source_target_pairs={{0,64},{64,0},{128,192},{192,128},{256,320},{320,256},{384,448},{4... | collective-permute-start | bytes 82952 | tf_op jit(solution)/shard_map/ppermute | solution.py:43
  154.8 4.1 %collective-permute-done.1 = f32[3,192,12]{1,2,0:T(8,128)S(1)} collective-permute-done((f32[3,192,12]{1,2,0:T(8,128)S(1)}, f32[3,192,12]{1,2,0:T(8,128)S(1)}, u32[]{:S(2)}, u32[]{:S(2)}) %collective-permute-start.1) | collective-permute-done | bytes 27680 | tf_op jit(solution)/shard_map/ppermute | solution.py:43
  158.9 2.8 %collective-permute-start.2 = (f32[3,192,12]{1,2,0:T(8,128)S(1)}, f32[3,192,12]{1,2,0:T(8,128)S(1)}, u32[]{:S(2)}, u32[]{:S(2)}) collective-permute-start(f32[3,192,12]{1,2,0:T(8,128)S(1)} %fusion.10), channel_id=1, source_target_pairs={{0,128},{64,192},{128,0},{192,64},{256,384},{320,448},{384,256},{4... | collective-permute-start | bytes 82952 | tf_op jit(solution)/shard_map/ppermute | solution.py:43
  161.7 3.1 %collective-permute-done.2 = f32[3,192,12]{1,2,0:T(8,128)S(1)} collective-permute-done((f32[3,192,12]{1,2,0:T(8,128)S(1)}, f32[3,192,12]{1,2,0:T(8,128)S(1)}, u32[]{:S(2)}, u32[]{:S(2)}) %collective-permute-start.2) | collective-permute-done | bytes 27680 | tf_op jit(solution)/shard_map/ppermute | solution.py:43
  164.9 6.8 %collective-permute-start.3 = (f32[3,192,12]{1,2,0:T(8,128)S(1)}, f32[3,192,12]{1,2,0:T(8,128)S(1)}, u32[]{:S(2)}, u32[]{:S(2)}) collective-permute-start(f32[3,192,12]{1,2,0:T(8,128)S(1)} %fusion.14), channel_id=1, source_target_pairs={{0,256},{64,320},{128,384},{192,448},{256,0},{320,64},{384,128},{4... | collective-permute-start | bytes 82952 | tf_op jit(solution)/shard_map/ppermute | solution.py:43
  171.7 2.1 %collective-permute-done.3 = f32[3,192,12]{1,2,0:T(8,128)S(1)} collective-permute-done((f32[3,192,12]{1,2,0:T(8,128)S(1)}, f32[3,192,12]{1,2,0:T(8,128)S(1)}, u32[]{:S(2)}, u32[]{:S(2)}) %collective-permute-start.3) | collective-permute-done | bytes 27680 | tf_op jit(solution)/shard_map/ppermute | solution.py:43
  173.8 11.9 %collective-permute-start.4 = (f32[3,192,12]{1,2,0:T(8,128)S(1)}, f32[3,192,12]{1,2,0:T(8,128)S(1)}, u32[]{:S(2)}, u32[]{:S(2)}) collective-permute-start(f32[3,192,12]{1,2,0:T(8,128)S(1)} %add.30), channel_id=1, source_target_pairs={{0,512},{64,576},{128,640},{192,704},{256,768},{320,832},{384,896}... | collective-permute-start | bytes 82952 | tf_op jit(solution)/shard_map/ppermute | solution.py:43
  185.6 2.7 %collective-permute-done.4 = f32[3,192,12]{1,2,0:T(8,128)S(1)} collective-permute-done((f32[3,192,12]{1,2,0:T(8,128)S(1)}, f32[3,192,12]{1,2,0:T(8,128)S(1)}, u32[]{:S(2)}, u32[]{:S(2)}) %collective-permute-start.4) | collective-permute-done | bytes 27680 | tf_op jit(solution)/shard_map/ppermute | solution.py:43
  (25 shorter events, 7.2 us)
Async XLA Ops:
  0.0 5.2 %copy-start = (bf16[3,512,192]{1,2,0:T(8,128)(2,1)S(1)}, bf16[3,512,192]{1,2,0:T(8,128)(2,1)}, u32[]{:S(2)}) copy-start(bf16[3,512,192]{1,2,0:T(8,128)(2,1)} %param.6) | copy-start | bytes 1769476
  17.3 4.7 %collective-permute-start = (f32[32,3,192,12]{2,0,3,1:T(8,128)S(1)}, f32[32,3,192,12]{2,0,3,1:T(8,128)S(1)}, u32[]{:S(2)}, u32[]{:S(2)}) collective-permute-start(f32[32,3,192,12]{2,0,3,1:T(8,128)S(1)} %select_bitcast_fusion), channel_id=1, source_target_pairs={{0,1},{1,0},{2,3},{3,2},{4,5},{5,4},{6,7},{7,6},{8,9},{9,8},{10,11... | collective-permute-start | bytes 2654216 | tf_op jit(solution)/shard_map/ppermute | solution.py:24
  24.4 17.0 %copy-start.2 = (s32[1,3]{1,0:T(1,128)S(1)}, s32[1,3]{1,0:T(1,128)}, u32[]{:S(2)}) copy-start(s32[1,3]{1,0:T(1,128)} %param.7) | copy-start | bytes 40
  24.4 56.1 %all-to-all-start = ((f32[32,3,192,12]{2,3,1,0:T(8,128)}), f32[32,3,192,12]{2,3,1,0:T(8,128)S(1)}, u32[]{:S(2)}, u32[]{:S(2)}) async-start(f32[32,3,192,12]{2,3,1,0:T(8,128)} %copy.33), calls=%async_computation | async-start | bytes 3145728 | tf_op jit(solution)/shard_map/all_to_all | solution.py:25
  80.6 12.1 %copy-start.1 = (bf16[1,768,768]{2,1,0:T(8,128)(2,1)S(1)}, bf16[1,768,768]{2,1,0:T(8,128)(2,1)}, u32[]{:S(2)}) copy-start(bf16[1,768,768]{2,1,0:T(8,128)(2,1)} %param.8) | copy-start | bytes 3538948
  81.7 31.2 %all-to-all-start.1 = ((bf16[64,192,12]{1,2,0:T(8,128)(2,1)}), bf16[64,192,12]{1,2,0:T(8,128)(2,1)S(1)}, u32[]{:S(2)}, u32[]{:S(2)}) async-start(bf16[64,192,12]{1,2,0:T(8,128)(2,1)} %select_select_fusion), calls=%async_computation.1 | async-start | bytes 1048576 | tf_op jit(solution)/shard_map/all_to_all | solution.py:31
  93.3 19.8 %copy-start.3 = (bf16[1,192,192]{2,1,0:T(8,128)(2,1)S(1)}, bf16[1,192,192]{2,1,0:T(8,128)(2,1)}, u32[]{:S(2)}) copy-start(bf16[1,192,192]{2,1,0:T(8,128)(2,1)} %param.9) | copy-start | bytes 221188
  116.8 36.0 %all-to-all-start.2 = ((f32[64,192,12]{1,2,0:T(8,128)}), f32[64,192,12]{1,2,0:T(8,128)S(1)}, u32[]{:S(2)}, u32[]{:S(2)}) async-start(f32[64,192,12]{1,2,0:T(8,128)} %copy.36), calls=%async_computation.2 | async-start | bytes 2097152 | tf_op jit(solution)/shard_map/all_to_all | solution.py:36
  152.9 6.0 %collective-permute-start.1 = (f32[3,192,12]{1,2,0:T(8,128)S(1)}, f32[3,192,12]{1,2,0:T(8,128)S(1)}, u32[]{:S(2)}, u32[]{:S(2)}) collective-permute-start(f32[3,192,12]{1,2,0:T(8,128)S(1)} %pad_maximum_fusion), channel_id=1, source_target_pairs={{0,64},{64,0},{128,192},{192,128},{256,320},{320,256},{384,448},{4... | collective-permute-start | bytes 82952 | tf_op jit(solution)/shard_map/ppermute | solution.py:43
  158.9 6.0 %collective-permute-start.2 = (f32[3,192,12]{1,2,0:T(8,128)S(1)}, f32[3,192,12]{1,2,0:T(8,128)S(1)}, u32[]{:S(2)}, u32[]{:S(2)}) collective-permute-start(f32[3,192,12]{1,2,0:T(8,128)S(1)} %fusion.10), channel_id=1, source_target_pairs={{0,128},{64,192},{128,0},{192,64},{256,384},{320,448},{384,256},{4... | collective-permute-start | bytes 82952 | tf_op jit(solution)/shard_map/ppermute | solution.py:43
  164.9 8.9 %collective-permute-start.3 = (f32[3,192,12]{1,2,0:T(8,128)S(1)}, f32[3,192,12]{1,2,0:T(8,128)S(1)}, u32[]{:S(2)}, u32[]{:S(2)}) collective-permute-start(f32[3,192,12]{1,2,0:T(8,128)S(1)} %fusion.14), channel_id=1, source_target_pairs={{0,256},{64,320},{128,384},{192,448},{256,0},{320,64},{384,128},{4... | collective-permute-start | bytes 82952 | tf_op jit(solution)/shard_map/ppermute | solution.py:43
  173.8 14.6 %collective-permute-start.4 = (f32[3,192,12]{1,2,0:T(8,128)S(1)}, f32[3,192,12]{1,2,0:T(8,128)S(1)}, u32[]{:S(2)}, u32[]{:S(2)}) collective-permute-start(f32[3,192,12]{1,2,0:T(8,128)S(1)} %add.30), channel_id=1, source_target_pairs={{0,512},{64,576},{128,640},{192,704},{256,768},{320,832},{384,896}... | collective-permute-start | bytes 82952 | tf_op jit(solution)/shard_map/ppermute | solution.py:43

commit v4 on v3

--- a/solution.py
+++ b/solution.py
@@ -16,11 +16,11 @@
     width = hid // members
     member = lax.axis_index(MEM)
     core = lax.axis_index("core")
-    blocks = act.reshape(layers, rows, members, width)
-    local = jnp.einsum("lrd,lrmc->mldc", cot, blocks, preferred_element_type=jnp.float32)
-    local = local.reshape(members // cores, cores, layers, dim, width)
-    keep = jnp.where(core == 0, local[:, 0], local[:, 1])
-    send = jnp.where(core == 0, local[:, 1], local[:, 0])
+    blocks = act.reshape(layers, rows, members // cores, cores, width)
+    mine_cols = lax.dynamic_index_in_dim(blocks, core, 3, keepdims=False)
+    other_cols = lax.dynamic_index_in_dim(blocks, 1 - core, 3, keepdims=False)
+    keep = jnp.einsum("lrd,lrmc->mldc", cot, mine_cols, preferred_element_type=jnp.float32)
+    send = jnp.einsum("lrd,lrmc->mldc", cot, other_cols, preferred_element_type=jnp.float32)
     pair = keep + lax.ppermute(send, "core", [(0, 1), (1, 0)])
     parts = lax.all_to_all(pair, CHIPS, 0, 0, tiled=True)
     shard = jnp.sum(parts, axis=0).astype(jnp.bfloat16)

time: 190 us -> 181 us (0.953)
  local copies, waits for them, and re-layouts: 18.6 us -> 13.5 us
  matrix products: 6.83 us -> 4.22 us
    slice x1 -> x0, local copies, waits for them, and re-layouts: 4.83 us -> none  [shards(): keep = jnp.where(core == 0, local[:, 0], local[:, 1])]
    dot_general x1 -> x2, matrix products: 4.57 us -> 1.96 us  [the longest x1 1 us: shards(): jnp.einsum('lrd,lrmc->mldc', cot, mine_cols, preferred_element_type=jnp.f...]
    reshape x2 -> x1, local copies, waits for them, and re-layouts: 4.81 us -> 2.34 us  [shards(): blocks = act.reshape(layers, rows, members // cores, cores, width)]
    dynamic_slice x0 -> x1, local copies, waits for them, and re-layouts: none -> 2.21 us  [shards(): mine_cols = lax.dynamic_index_in_dim(blocks, core, 3, keepdims=False)]
where the time goes in v4:
time: 181 us
  waiting for transfers between devices  95.2 us (53%)
  starting transfers between devices  57.9 us (32%)
  local copies, waits for them, and re-layouts  13.5 us (7%)
  between operations  5.87 us (3%)
  matrix products  4.22 us (2%)
  other arithmetic  3.79 us (2%)
    all_to_all x1, waiting for transfers between devices, shards(): parts = lax.all_to_all(pair, CHIPS, 0, 0, tiled=True)  36.6 us
    all_to_all x1, waiting for transfers between devices, shards(): returned = lax.all_to_all(pieces, MEM, 0, 0, tiled=True)  25.2 us
    ppermute x4, starting transfers between devices, shards(): total = total + lax.ppermute(total, 'grp', pairs)  22.9 us
    all_to_all x1, waiting for transfers between devices, shards(): gathered = lax.all_to_all(outgoing, MEM, 0, 0, tiled=True)  18.2 us
    all_to_all x1, starting transfers between devices, shards(): parts = lax.all_to_all(pair, CHIPS, 0, 0, tiled=True)  17 us
    ppermute x4, waiting for transfers between devices, shards(): total = total + lax.ppermute(total, 'grp', pairs)  12.4 us
    all_to_all x1, starting transfers between devices, shards(): gathered = lax.all_to_all(outgoing, MEM, 0, 0, tiled=True)  11 us
    all_to_all x1, starting transfers between devices, shards(): returned = lax.all_to_all(pieces, MEM, 0, 0, tiled=True)  5.16 us
  transfers between devices with their start and end apart: 8, of which 8 were waited for; matrix products, arithmetic and copies ran while one was open for 2% of the time, Pallas kernels for 0%

profile of v4, /device:TPU:4, one launch (start us, length us, event | category | flops | bytes accessed | tf_op | source)
XLA Modules:
  0.0 180.6 jit_solution(16894198656870537947)
XLA Ops:
  0.0 2.9 %copy.16 = bf16[3,512,768]{1,2,0:T(8,128)(2,1)S(1)} copy(bf16[3,512,768]{2,1,0:T(8,128)(2,1)} %param.5) | data formatting | bytes 4718592 | tf_op args[0]
  2.9 2.3 %reshape.23 = bf16[3,512,32,2,12]{1,4,3,2,0:T(8,128)(2,1)} reshape(bf16[3,512,768]{1,2,0:T(8,128)(2,1)S(1)} %copy.16) | data formatting | bytes 4718592 | tf_op jit(solution)/shard_map/reshape | solution.py:19
  5.2 2.2 %constant_dynamic-slice_fusion.4 = (bf16[3,512,32,1,12]{1,4,3,2,0:T(8,128)(2,1)S(1)}, bf16[3,512,32,1,12]{1,4,3,2,0:T(8,128)(2,1)S(1)}) fusion(bf16[3,512,32,2,12]{1,4,3,2,0:T(8,128)(2,1)} %reshape.23, s32[]{:T(128)S(6)} %select_n.26, s32[]{:T(128)S(6)} %select_n.27), kind=kLoop, calls=%fused_computation.24 | loop fusion | bytes 4718600 | tf_op jit(solution)/shard_map/jit(dynamic_index_in_dim)/dynamic_slice | solution.py:20
  8.4 1.9 %collective-permute-start = (f32[32,3,192,12]{2,0,3,1:T(8,128)S(1)}, f32[32,3,192,12]{2,0,3,1:T(8,128)S(1)}, u32[]{:S(2)}, u32[]{:S(2)}) collective-permute-start(f32[32,3,192,12]{2,0,3,1:T(8,128)S(1)} %convolution_bitcast_fusion), channel_id=1, source_target_pairs={{0,1},{1,0},{2,3},{3,2},{4,5},{5,4},{6,7},{7,6},{8,9},{9,8},{10,11... | collective-permute-start | bytes 2654216 | tf_op jit(solution)/shard_map/ppermute | solution.py:24
  10.4 2.8 %collective-permute-done = f32[32,3,192,12]{2,0,3,1:T(8,128)S(1)} collective-permute-done((f32[32,3,192,12]{2,0,3,1:T(8,128)S(1)}, f32[32,3,192,12]{2,0,3,1:T(8,128)S(1)}, u32[]{:S(2)}, u32[]{:S(2)}) %collective-permute-start) | collective-permute-done | bytes 884768 | tf_op jit(solution)/shard_map/ppermute | solution.py:24
  14.2 1.9 %copy.19 = f32[32,3,192,12]{2,3,1,0:T(8,128)} copy(f32[32,3,192,12]{2,0,3,1:T(8,128)S(1)} %fusion) | data formatting | bytes 1769472 | tf_op jit(solution)/shard_map/add | solution.py:24
  16.1 17.0 %all-to-all-start = ((f32[32,3,192,12]{2,3,1,0:T(8,128)}), f32[32,3,192,12]{2,3,1,0:T(8,128)S(1)}, u32[]{:S(2)}, u32[]{:S(2)}) async-start(f32[32,3,192,12]{2,3,1,0:T(8,128)} %copy.19), calls=%async_computation | async-start | bytes 3145728 | tf_op jit(solution)/shard_map/all_to_all | solution.py:25
  34.3 1.2 iota_compare_fusion
  35.6 36.6 %all-to-all-done = f32[32,3,192,12]{2,3,1,0:T(8,128)S(1)} async-done(((f32[32,3,192,12]{2,3,1,0:T(8,128)}), f32[32,3,192,12]{2,3,1,0:T(8,128)S(1)}, u32[]{:S(2)}, u32[]{:S(2)}) %all-to-all-start) | async-done | bytes 884768 | tf_op jit(solution)/shard_map/all_to_all | solution.py:25
  73.4 11.0 %all-to-all-start.1 = ((bf16[64,192,12]{1,2,0:T(8,128)(2,1)}), bf16[64,192,12]{1,2,0:T(8,128)(2,1)S(1)}, u32[]{:S(2)}, u32[]{:S(2)}) async-start(bf16[64,192,12]{1,2,0:T(8,128)(2,1)} %select_select_fusion), calls=%async_computation.1 | async-start | bytes 1048576 | tf_op jit(solution)/shard_map/all_to_all | solution.py:31
  85.1 1.3 dot_general.20
  86.4 18.2 %all-to-all-done.1 = bf16[64,192,12]{1,2,0:T(8,128)(2,1)S(1)} async-done(((bf16[64,192,12]{1,2,0:T(8,128)(2,1)}), bf16[64,192,12]{1,2,0:T(8,128)(2,1)S(1)}, u32[]{:S(2)}, u32[]{:S(2)}) %all-to-all-start.1) | async-done | bytes 294944 | tf_op jit(solution)/shard_map/all_to_all | solution.py:31
  104.8 2.3 %convolution_bitcast_fusion.2 = f32[64,192,12]{1,0,2:T(8,128)S(1)} fusion(bf16[64,12,768]{2,1,0:T(8,128)(2,1)} %dot_general.20, bf16[192,768]{0,1:T(8,128)(2,1)S(1)} %reshape.24, bf16[1,192,192]{2,1,0:T(8,128)(2,1)S(1)} %copy-done.3), kind=kOutput, calls=%fused_computation.3 | convolution fusion | flops 283262976 | bytes 2138112 | tf_op jit(solution)/shard_map/dot_general | solution.py:34
  107.1 1.5 copy.22
  108.6 5.2 %all-to-all-start.2 = ((f32[64,192,12]{1,2,0:T(8,128)}), f32[64,192,12]{1,2,0:T(8,128)S(1)}, u32[]{:S(2)}, u32[]{:S(2)}) async-start(f32[64,192,12]{1,2,0:T(8,128)} %copy.22), calls=%async_computation.2 | async-start | bytes 2097152 | tf_op jit(solution)/shard_map/all_to_all | solution.py:36
  119.4 25.2 %all-to-all-done.2 = f32[64,192,12]{1,2,0:T(8,128)S(1)} async-done(((f32[64,192,12]{1,2,0:T(8,128)}), f32[64,192,12]{1,2,0:T(8,128)S(1)}, u32[]{:S(2)}, u32[]{:S(2)}) %all-to-all-start.2) | async-done | bytes 589856 | tf_op jit(solution)/shard_map/all_to_all | solution.py:36
  144.6 1.9 %collective-permute-start.1 = (f32[3,192,12]{1,2,0:T(8,128)S(1)}, f32[3,192,12]{1,2,0:T(8,128)S(1)}, u32[]{:S(2)}, u32[]{:S(2)}) collective-permute-start(f32[3,192,12]{1,2,0:T(8,128)S(1)} %pad_maximum_fusion), channel_id=1, source_target_pairs={{0,64},{64,0},{128,192},{192,128},{256,320},{320,256},{384,448},{4... | collective-permute-start | bytes 82952 | tf_op jit(solution)/shard_map/ppermute | solution.py:43
  146.5 4.1 %collective-permute-done.1 = f32[3,192,12]{1,2,0:T(8,128)S(1)} collective-permute-done((f32[3,192,12]{1,2,0:T(8,128)S(1)}, f32[3,192,12]{1,2,0:T(8,128)S(1)}, u32[]{:S(2)}, u32[]{:S(2)}) %collective-permute-start.1) | collective-permute-done | bytes 27680 | tf_op jit(solution)/shard_map/ppermute | solution.py:43
  150.6 2.4 %collective-permute-start.2 = (f32[3,192,12]{1,2,0:T(8,128)S(1)}, f32[3,192,12]{1,2,0:T(8,128)S(1)}, u32[]{:S(2)}, u32[]{:S(2)}) collective-permute-start(f32[3,192,12]{1,2,0:T(8,128)S(1)} %fusion.11), channel_id=1, source_target_pairs={{0,128},{64,192},{128,0},{192,64},{256,384},{320,448},{384,256},{4... | collective-permute-start | bytes 82952 | tf_op jit(solution)/shard_map/ppermute | solution.py:43
  153.0 3.6 %collective-permute-done.2 = f32[3,192,12]{1,2,0:T(8,128)S(1)} collective-permute-done((f32[3,192,12]{1,2,0:T(8,128)S(1)}, f32[3,192,12]{1,2,0:T(8,128)S(1)}, u32[]{:S(2)}, u32[]{:S(2)}) %collective-permute-start.2) | collective-permute-done | bytes 27680 | tf_op jit(solution)/shard_map/ppermute | solution.py:43
  156.6 6.9 %collective-permute-start.3 = (f32[3,192,12]{1,2,0:T(8,128)S(1)}, f32[3,192,12]{1,2,0:T(8,128)S(1)}, u32[]{:S(2)}, u32[]{:S(2)}) collective-permute-start(f32[3,192,12]{1,2,0:T(8,128)S(1)} %fusion.14), channel_id=1, source_target_pairs={{0,256},{64,320},{128,384},{192,448},{256,0},{320,64},{384,128},{4... | collective-permute-start | bytes 82952 | tf_op jit(solution)/shard_map/ppermute | solution.py:43
  163.5 2.1 %collective-permute-done.3 = f32[3,192,12]{1,2,0:T(8,128)S(1)} collective-permute-done((f32[3,192,12]{1,2,0:T(8,128)S(1)}, f32[3,192,12]{1,2,0:T(8,128)S(1)}, u32[]{:S(2)}, u32[]{:S(2)}) %collective-permute-start.3) | collective-permute-done | bytes 27680 | tf_op jit(solution)/shard_map/ppermute | solution.py:43
  165.5 11.7 %collective-permute-start.4 = (f32[3,192,12]{1,2,0:T(8,128)S(1)}, f32[3,192,12]{1,2,0:T(8,128)S(1)}, u32[]{:S(2)}, u32[]{:S(2)}) collective-permute-start(f32[3,192,12]{1,2,0:T(8,128)S(1)} %add.40), channel_id=1, source_target_pairs={{0,512},{64,576},{128,640},{192,704},{256,768},{320,832},{384,896}... | collective-permute-start | bytes 82952 | tf_op jit(solution)/shard_map/ppermute | solution.py:43
  177.3 2.7 %collective-permute-done.4 = f32[3,192,12]{1,2,0:T(8,128)S(1)} collective-permute-done((f32[3,192,12]{1,2,0:T(8,128)S(1)}, f32[3,192,12]{1,2,0:T(8,128)S(1)}, u32[]{:S(2)}, u32[]{:S(2)}) %collective-permute-start.4) | collective-permute-done | bytes 27680 | tf_op jit(solution)/shard_map/ppermute | solution.py:43
  (23 shorter events, 6.0 us)
Async XLA Ops:
  0.0 7.5 %copy-start = (bf16[3,512,192]{1,2,0:T(8,128)(2,1)S(1)}, bf16[3,512,192]{1,2,0:T(8,128)(2,1)}, u32[]{:S(2)}) copy-start(bf16[3,512,192]{1,2,0:T(8,128)(2,1)} %param.6) | copy-start | bytes 1769476
  8.4 4.7 %collective-permute-start = (f32[32,3,192,12]{2,0,3,1:T(8,128)S(1)}, f32[32,3,192,12]{2,0,3,1:T(8,128)S(1)}, u32[]{:S(2)}, u32[]{:S(2)}) collective-permute-start(f32[32,3,192,12]{2,0,3,1:T(8,128)S(1)} %convolution_bitcast_fusion), channel_id=1, source_target_pairs={{0,1},{1,0},{2,3},{3,2},{4,5},{5,4},{6,7},{7,6},{8,9},{9,8},{10,11... | collective-permute-start | bytes 2654216 | tf_op jit(solution)/shard_map/ppermute | solution.py:24
  16.1 17.0 %copy-start.2 = (s32[1,3]{1,0:T(1,128)S(1)}, s32[1,3]{1,0:T(1,128)}, u32[]{:S(2)}) copy-start(s32[1,3]{1,0:T(1,128)} %param.7) | copy-start | bytes 40
  16.1 56.1 %all-to-all-start = ((f32[32,3,192,12]{2,3,1,0:T(8,128)}), f32[32,3,192,12]{2,3,1,0:T(8,128)S(1)}, u32[]{:S(2)}, u32[]{:S(2)}) async-start(f32[32,3,192,12]{2,3,1,0:T(8,128)} %copy.19), calls=%async_computation | async-start | bytes 3145728 | tf_op jit(solution)/shard_map/all_to_all | solution.py:25
  35.5 48.9 %copy-start.1 = (bf16[1,768,768]{2,1,0:T(8,128)(2,1)S(1)}, bf16[1,768,768]{2,1,0:T(8,128)(2,1)}, u32[]{:S(2)}) copy-start(bf16[1,768,768]{2,1,0:T(8,128)(2,1)} %param.8) | copy-start | bytes 3538948
  73.4 31.2 %all-to-all-start.1 = ((bf16[64,192,12]{1,2,0:T(8,128)(2,1)}), bf16[64,192,12]{1,2,0:T(8,128)(2,1)S(1)}, u32[]{:S(2)}, u32[]{:S(2)}) async-start(bf16[64,192,12]{1,2,0:T(8,128)(2,1)} %select_select_fusion), calls=%async_computation.1 | async-start | bytes 1048576 | tf_op jit(solution)/shard_map/all_to_all | solution.py:31
  85.1 19.8 %copy-start.3 = (bf16[1,192,192]{2,1,0:T(8,128)(2,1)S(1)}, bf16[1,192,192]{2,1,0:T(8,128)(2,1)}, u32[]{:S(2)}) copy-start(bf16[1,192,192]{2,1,0:T(8,128)(2,1)} %param.9) | copy-start | bytes 221188
  108.6 36.0 %all-to-all-start.2 = ((f32[64,192,12]{1,2,0:T(8,128)}), f32[64,192,12]{1,2,0:T(8,128)S(1)}, u32[]{:S(2)}, u32[]{:S(2)}) async-start(f32[64,192,12]{1,2,0:T(8,128)} %copy.22), calls=%async_computation.2 | async-start | bytes 2097152 | tf_op jit(solution)/shard_map/all_to_all | solution.py:36
  144.6 6.0 %collective-permute-start.1 = (f32[3,192,12]{1,2,0:T(8,128)S(1)}, f32[3,192,12]{1,2,0:T(8,128)S(1)}, u32[]{:S(2)}, u32[]{:S(2)}) collective-permute-start(f32[3,192,12]{1,2,0:T(8,128)S(1)} %pad_maximum_fusion), channel_id=1, source_target_pairs={{0,64},{64,0},{128,192},{192,128},{256,320},{320,256},{384,448},{4... | collective-permute-start | bytes 82952 | tf_op jit(solution)/shard_map/ppermute | solution.py:43
  150.6 6.0 %collective-permute-start.2 = (f32[3,192,12]{1,2,0:T(8,128)S(1)}, f32[3,192,12]{1,2,0:T(8,128)S(1)}, u32[]{:S(2)}, u32[]{:S(2)}) collective-permute-start(f32[3,192,12]{1,2,0:T(8,128)S(1)} %fusion.11), channel_id=1, source_target_pairs={{0,128},{64,192},{128,0},{192,64},{256,384},{320,448},{384,256},{4... | collective-permute-start | bytes 82952 | tf_op jit(solution)/shard_map/ppermute | solution.py:43
  156.6 8.9 %collective-permute-start.3 = (f32[3,192,12]{1,2,0:T(8,128)S(1)}, f32[3,192,12]{1,2,0:T(8,128)S(1)}, u32[]{:S(2)}, u32[]{:S(2)}) collective-permute-start(f32[3,192,12]{1,2,0:T(8,128)S(1)} %fusion.14), channel_id=1, source_target_pairs={{0,256},{64,320},{128,384},{192,448},{256,0},{320,64},{384,128},{4... | collective-permute-start | bytes 82952 | tf_op jit(solution)/shard_map/ppermute | solution.py:43
  165.5 14.4 %collective-permute-start.4 = (f32[3,192,12]{1,2,0:T(8,128)S(1)}, f32[3,192,12]{1,2,0:T(8,128)S(1)}, u32[]{:S(2)}, u32[]{:S(2)}) collective-permute-start(f32[3,192,12]{1,2,0:T(8,128)S(1)} %add.40), channel_id=1, source_target_pairs={{0,512},{64,576},{128,640},{192,704},{256,768},{320,832},{384,896}... | collective-permute-start | bytes 82952 | tf_op jit(solution)/shard_map/ppermute | solution.py:43

commit v5 on v4

--- a/solution.py
+++ b/solution.py
@@ -16,20 +16,21 @@
     width = hid // members
     member = lax.axis_index(MEM)
     core = lax.axis_index("core")
-    blocks = act.reshape(layers, rows, members // cores, cores, width)
-    mine_cols = lax.dynamic_index_in_dim(blocks, core, 3, keepdims=False)
-    other_cols = lax.dynamic_index_in_dim(blocks, 1 - core, 3, keepdims=False)
-    keep = jnp.einsum("lrd,lrmc->mldc", cot, mine_cols, preferred_element_type=jnp.float32)
-    send = jnp.einsum("lrd,lrmc->mldc", cot, other_cols, preferred_element_type=jnp.float32)
+    height = dim // members
+    blocks = cot.reshape(layers, rows, members // cores, cores, height)
+    mine_rows = lax.dynamic_index_in_dim(blocks, core, 3, keepdims=False)
+    other_rows = lax.dynamic_index_in_dim(blocks, 1 - core, 3, keepdims=False)
+    keep = jnp.einsum("lrmk,lrh->mlkh", mine_rows, act, preferred_element_type=jnp.float32)
+    send = jnp.einsum("lrmk,lrh->mlkh", other_rows, act, preferred_element_type=jnp.float32)
     pair = keep + lax.ppermute(send, "core", [(0, 1), (1, 0)])
     parts = lax.all_to_all(pair, CHIPS, 0, 0, tiled=True)
     shard = jnp.sum(parts, axis=0).astype(jnp.bfloat16)
     slots = lax.broadcasted_iota(jnp.int32, (members, 1, 1), 0)
-    outgoing = jnp.zeros((members, dim, width), jnp.bfloat16)
+    outgoing = jnp.zeros((members, height, hid), jnp.bfloat16)
     for layer in range(layers):
         outgoing = jnp.where(slots == owner[0, layer], shard[layer][None], outgoing)
     gathered = lax.all_to_all(outgoing, MEM, 0, 0, tiled=True)
-    grad = jnp.transpose(gathered, (1, 0, 2)).reshape(dim, hid)
+    grad = gathered.reshape(dim, hid)
     left = jnp.dot(g_inverse[0], grad, preferred_element_type=jnp.float32).astype(jnp.bfloat16)
     term = jnp.dot(left, a_inverse[0], preferred_element_type=jnp.float32)
     pieces = jnp.transpose(term.reshape(dim, members, width), (1, 0, 2))

time: 181 us -> 163 us (0.901)
  waiting for transfers between devices: 95.2 us -> 83.7 us
  starting transfers between devices: 57.9 us -> 54.5 us
  local copies, waits for them, and re-layouts: 13.5 us -> 10.4 us
    all_to_all x1, waiting for transfers between devices: 36.6 us -> 28.5 us  [shards(): parts = lax.all_to_all(pair, CHIPS, 0, 0, tiled=True)]
    all_to_all x1, waiting for transfers between devices: 18.2 us -> 14.5 us  [shards(): gathered = lax.all_to_all(outgoing, MEM, 0, 0, tiled=True)]
    unnamed x9 -> x4, local copies, waits for them, and re-layouts: 2.92 us -> 0.08 us
    all_to_all x1, starting transfers between devices: 11 us -> 9.03 us  [shards(): gathered = lax.all_to_all(outgoing, MEM, 0, 0, tiled=True)]
    dynamic_slice x1, local copies, waits for them, and re-layouts: 2.21 us -> 0.28 us  [shards(): mine_rows = lax.dynamic_index_in_dim(blocks, core, 3, keepdims=False)]
  transfers between devices with their start and end apart: 8 -> 8, of which waited for: 8 -> 8; matrix products, arithmetic and copies ran while one was open for 2% -> 3% of each run, Pallas kernels for 0% -> 0%
where the time goes in v5:
time: 163 us; the launch traced here: 162 us
  waiting for transfers between devices  83.7 us (51%)
  starting transfers between devices  54.5 us (33%)
  local copies, waits for them, and re-layouts  10.4 us (6%)
  between operations  5.57 us (3%)
  other arithmetic  4.4 us (3%)
  matrix products  3.19 us (2%)
    all_to_all x1, waiting for transfers between devices, shards(): parts = lax.all_to_all(pair, CHIPS, 0, 0, tiled=True)  28.5 us
    all_to_all x1, waiting for transfers between devices, shards(): returned = lax.all_to_all(pieces, MEM, 0, 0, tiled=True)  25.4 us
    ppermute x4, starting transfers between devices, shards(): total = total + lax.ppermute(total, 'grp', pairs)  21.6 us
    all_to_all x1, starting transfers between devices, shards(): parts = lax.all_to_all(pair, CHIPS, 0, 0, tiled=True)  16.9 us
    all_to_all x1, waiting for transfers between devices, shards(): gathered = lax.all_to_all(outgoing, MEM, 0, 0, tiled=True)  14.5 us
    ppermute x4, waiting for transfers between devices, shards(): total = total + lax.ppermute(total, 'grp', pairs)  12.8 us
    all_to_all x1, starting transfers between devices, shards(): gathered = lax.all_to_all(outgoing, MEM, 0, 0, tiled=True)  9.03 us
    all_to_all x1, starting transfers between devices, shards(): returned = lax.all_to_all(pieces, MEM, 0, 0, tiled=True)  5.08 us
  transfers between devices with their start and end apart: 8, of which 8 were waited for; matrix products, arithmetic and copies ran while one was open for 3% of the time, Pallas kernels for 0%

profile of v5, /device:TPU:4, one launch (start us, length us, event | category | flops | bytes accessed | tf_op | source)
XLA Modules:
  0.0 161.9 jit_solution(943345088778474660)
XLA Ops:
  0.0 1.5 reshape.23
  2.3 1.9 %collective-permute-start = (f32[32,3,3,768]{3,0,2,1:T(8,128)S(1)}, f32[32,3,3,768]{3,0,2,1:T(8,128)S(1)}, u32[]{:S(2)}, u32[]{:S(2)}) collective-permute-start(f32[32,3,3,768]{3,0,2,1:T(8,128)S(1)} %fusion.7), channel_id=1, source_target_pairs={{0,1},{1,0},{2,3},{3,2},{4,5},{5,4},{6,7},{7,6},{8,9},{9,8},{10,11... | collective-permute-start | bytes 2654216 | tf_op jit(solution)/shard_map/ppermute | solution.py:25
  4.3 2.4 %collective-permute-done = f32[32,3,3,768]{3,0,2,1:T(8,128)S(1)} collective-permute-done((f32[32,3,3,768]{3,0,2,1:T(8,128)S(1)}, f32[32,3,3,768]{3,0,2,1:T(8,128)S(1)}, u32[]{:S(2)}, u32[]{:S(2)}) %collective-permute-start) | collective-permute-done | bytes 884768 | tf_op jit(solution)/shard_map/ppermute | solution.py:25
  7.2 1.6 %copy.17 = f32[32,3,3,768]{3,2,1,0:T(4,128)} copy(f32[32,3,3,768]{3,0,2,1:T(8,128)S(1)} %fusion.10) | data formatting | bytes 1769472 | tf_op jit(solution)/shard_map/add | solution.py:25
  8.8 16.9 %all-to-all-start = ((f32[32,3,3,768]{3,2,1,0:T(4,128)}), f32[32,3,3,768]{3,2,1,0:T(4,128)S(1)}, u32[]{:S(2)}, u32[]{:S(2)}) async-start(f32[32,3,3,768]{3,2,1,0:T(4,128)} %copy.17), calls=%async_computation | async-start | bytes 2359296 | tf_op jit(solution)/shard_map/all_to_all | solution.py:26
  27.1 1.2 iota_compare_fusion
  28.2 28.5 %all-to-all-done = f32[32,3,3,768]{3,2,1,0:T(4,128)S(1)} async-done(((f32[32,3,3,768]{3,2,1,0:T(4,128)}), f32[32,3,3,768]{3,2,1,0:T(4,128)S(1)}, u32[]{:S(2)}, u32[]{:S(2)}) %all-to-all-start) | async-done | bytes 884768 | tf_op jit(solution)/shard_map/all_to_all | solution.py:26
  59.4 9.0 %all-to-all-start.1 = ((bf16[64,3,768]{2,1,0:T(4,128)(2,1)}), bf16[64,3,768]{2,1,0:T(4,128)(2,1)}, u32[]{:S(2)}, u32[]{:S(2)}) async-start(bf16[64,3,768]{2,1,0:T(4,128)(2,1)} %select_select_fusion), calls=%async_computation.1 | async-start | bytes 786432 | tf_op jit(solution)/shard_map/all_to_all | solution.py:32
  68.4 1.6 copy.18
  70.0 1.3 dot_general.20
  71.3 14.5 %all-to-all-done.1 = bf16[64,3,768]{2,1,0:T(4,128)(2,1)} async-done(((bf16[64,3,768]{2,1,0:T(4,128)(2,1)}), bf16[64,3,768]{2,1,0:T(4,128)(2,1)}, u32[]{:S(2)}, u32[]{:S(2)}) %all-to-all-start.1) | async-done | bytes 294944 | tf_op jit(solution)/shard_map/all_to_all | solution.py:32
  85.9 1.2 reshape.24
  87.1 2.2 %convolution_bitcast_fusion = f32[64,192,12]{1,0,2:T(8,128)S(1)} fusion(bf16[64,12,768]{2,1,0:T(8,128)(2,1)} %dot_general.20, bf16[192,768]{1,0:T(8,128)(2,1)S(1)} %reshape.24, bf16[1,192,192]{2,1,0:T(8,128)(2,1)} %param.9), kind=kOutput, calls=%fused_computation.7 | convolution fusion | flops 283262976 | bytes 2138112 | tf_op jit(solution)/shard_map/dot_general | solution.py:35
  89.3 1.4 copy.20
  90.8 5.1 %all-to-all-start.2 = ((f32[64,192,12]{1,2,0:T(8,128)}), f32[64,192,12]{1,2,0:T(8,128)S(1)}, u32[]{:S(2)}, u32[]{:S(2)}) async-start(f32[64,192,12]{1,2,0:T(8,128)} %copy.20), calls=%async_computation.2 | async-start | bytes 2097152 | tf_op jit(solution)/shard_map/all_to_all | solution.py:37
  101.3 25.4 %all-to-all-done.2 = f32[64,192,12]{1,2,0:T(8,128)S(1)} async-done(((f32[64,192,12]{1,2,0:T(8,128)}), f32[64,192,12]{1,2,0:T(8,128)S(1)}, u32[]{:S(2)}, u32[]{:S(2)}) %all-to-all-start.2) | async-done | bytes 589856 | tf_op jit(solution)/shard_map/all_to_all | solution.py:37
  126.7 1.9 %collective-permute-start.1 = (f32[3,192,12]{1,2,0:T(8,128)S(1)}, f32[3,192,12]{1,2,0:T(8,128)S(1)}, u32[]{:S(2)}, u32[]{:S(2)}) collective-permute-start(f32[3,192,12]{1,2,0:T(8,128)S(1)} %pad_maximum_fusion), channel_id=1, source_target_pairs={{0,64},{64,0},{128,192},{192,128},{256,320},{320,256},{384,448},{4... | collective-permute-start | bytes 82952 | tf_op jit(solution)/shard_map/ppermute | solution.py:44
  128.7 4.1 %collective-permute-done.1 = f32[3,192,12]{1,2,0:T(8,128)S(1)} collective-permute-done((f32[3,192,12]{1,2,0:T(8,128)S(1)}, f32[3,192,12]{1,2,0:T(8,128)S(1)}, u32[]{:S(2)}, u32[]{:S(2)}) %collective-permute-start.1) | collective-permute-done | bytes 27680 | tf_op jit(solution)/shard_map/ppermute | solution.py:44
  132.7 1.9 %collective-permute-start.2 = (f32[3,192,12]{1,2,0:T(8,128)S(1)}, f32[3,192,12]{1,2,0:T(8,128)S(1)}, u32[]{:S(2)}, u32[]{:S(2)}) collective-permute-start(f32[3,192,12]{1,2,0:T(8,128)S(1)} %fusion.21), channel_id=1, source_target_pairs={{0,128},{64,192},{128,0},{192,64},{256,384},{320,448},{384,256},{4... | collective-permute-start | bytes 82952 | tf_op jit(solution)/shard_map/ppermute | solution.py:44
  134.7 4.1 %collective-permute-done.2 = f32[3,192,12]{1,2,0:T(8,128)S(1)} collective-permute-done((f32[3,192,12]{1,2,0:T(8,128)S(1)}, f32[3,192,12]{1,2,0:T(8,128)S(1)}, u32[]{:S(2)}, u32[]{:S(2)}) %collective-permute-start.2) | collective-permute-done | bytes 27680 | tf_op jit(solution)/shard_map/ppermute | solution.py:44
  138.7 5.9 %collective-permute-start.3 = (f32[3,192,12]{1,2,0:T(8,128)S(1)}, f32[3,192,12]{1,2,0:T(8,128)S(1)}, u32[]{:S(2)}, u32[]{:S(2)}) collective-permute-start(f32[3,192,12]{1,2,0:T(8,128)S(1)} %fusion.24), channel_id=1, source_target_pairs={{0,256},{64,320},{128,384},{192,448},{256,0},{320,64},{384,128},{4... | collective-permute-start | bytes 82952 | tf_op jit(solution)/shard_map/ppermute | solution.py:44
  144.6 2.1 %collective-permute-done.3 = f32[3,192,12]{1,2,0:T(8,128)S(1)} collective-permute-done((f32[3,192,12]{1,2,0:T(8,128)S(1)}, f32[3,192,12]{1,2,0:T(8,128)S(1)}, u32[]{:S(2)}, u32[]{:S(2)}) %collective-permute-start.3) | collective-permute-done | bytes 27680 | tf_op jit(solution)/shard_map/ppermute | solution.py:44
  146.7 11.9 %collective-permute-start.4 = (f32[3,192,12]{1,2,0:T(8,128)S(1)}, f32[3,192,12]{1,2,0:T(8,128)S(1)}, u32[]{:S(2)}, u32[]{:S(2)}) collective-permute-start(f32[3,192,12]{1,2,0:T(8,128)S(1)} %add.40), channel_id=1, source_target_pairs={{0,512},{64,576},{128,640},{192,704},{256,768},{320,832},{384,896}... | collective-permute-start | bytes 82952 | tf_op jit(solution)/shard_map/ppermute | solution.py:44
  158.6 2.7 %collective-permute-done.4 = f32[3,192,12]{1,2,0:T(8,128)S(1)} collective-permute-done((f32[3,192,12]{1,2,0:T(8,128)S(1)}, f32[3,192,12]{1,2,0:T(8,128)S(1)}, u32[]{:S(2)}, u32[]{:S(2)}) %collective-permute-start.4) | collective-permute-done | bytes 27680 | tf_op jit(solution)/shard_map/ppermute | solution.py:44
  (18 shorter events, 6.0 us)
Async XLA Ops:
  0.0 1.8 %copy-start = (bf16[3,512,768]{2,1,0:T(8,128)(2,1)S(1)}, bf16[3,512,768]{2,1,0:T(8,128)(2,1)}, u32[]{:S(2)}) copy-start(bf16[3,512,768]{2,1,0:T(8,128)(2,1)} %param.5) | copy-start | bytes 7077892
  2.3 4.3 %collective-permute-start = (f32[32,3,3,768]{3,0,2,1:T(8,128)S(1)}, f32[32,3,3,768]{3,0,2,1:T(8,128)S(1)}, u32[]{:S(2)}, u32[]{:S(2)}) collective-permute-start(f32[32,3,3,768]{3,0,2,1:T(8,128)S(1)} %fusion.7), channel_id=1, source_target_pairs={{0,1},{1,0},{2,3},{3,2},{4,5},{5,4},{6,7},{7,6},{8,9},{9,8},{10,11... | collective-permute-start | bytes 2654216 | tf_op jit(solution)/shard_map/ppermute | solution.py:25
  8.8 16.9 %copy-start.1 = (s32[1,3]{1,0:T(1,128)S(1)}, s32[1,3]{1,0:T(1,128)}, u32[]{:S(2)}) copy-start(s32[1,3]{1,0:T(1,128)} %param.7) | copy-start | bytes 40
  8.8 47.9 %all-to-all-start = ((f32[32,3,3,768]{3,2,1,0:T(4,128)}), f32[32,3,3,768]{3,2,1,0:T(4,128)S(1)}, u32[]{:S(2)}, u32[]{:S(2)}) async-start(f32[32,3,3,768]{3,2,1,0:T(4,128)} %copy.17), calls=%async_computation | async-start | bytes 2359296 | tf_op jit(solution)/shard_map/all_to_all | solution.py:26
  59.4 26.5 %all-to-all-start.1 = ((bf16[64,3,768]{2,1,0:T(4,128)(2,1)}), bf16[64,3,768]{2,1,0:T(4,128)(2,1)}, u32[]{:S(2)}, u32[]{:S(2)}) async-start(bf16[64,3,768]{2,1,0:T(4,128)(2,1)} %select_select_fusion), calls=%async_computation.1 | async-start | bytes 786432 | tf_op jit(solution)/shard_map/all_to_all | solution.py:32
  90.8 35.9 %all-to-all-start.2 = ((f32[64,192,12]{1,2,0:T(8,128)}), f32[64,192,12]{1,2,0:T(8,128)S(1)}, u32[]{:S(2)}, u32[]{:S(2)}) async-start(f32[64,192,12]{1,2,0:T(8,128)} %copy.20), calls=%async_computation.2 | async-start | bytes 2097152 | tf_op jit(solution)/shard_map/all_to_all | solution.py:37
  126.7 6.0 %collective-permute-start.1 = (f32[3,192,12]{1,2,0:T(8,128)S(1)}, f32[3,192,12]{1,2,0:T(8,128)S(1)}, u32[]{:S(2)}, u32[]{:S(2)}) collective-permute-start(f32[3,192,12]{1,2,0:T(8,128)S(1)} %pad_maximum_fusion), channel_id=1, source_target_pairs={{0,64},{64,0},{128,192},{192,128},{256,320},{320,256},{384,448},{4... | collective-permute-start | bytes 82952 | tf_op jit(solution)/shard_map/ppermute | solution.py:44
  132.7 6.0 %collective-permute-start.2 = (f32[3,192,12]{1,2,0:T(8,128)S(1)}, f32[3,192,12]{1,2,0:T(8,128)S(1)}, u32[]{:S(2)}, u32[]{:S(2)}) collective-permute-start(f32[3,192,12]{1,2,0:T(8,128)S(1)} %fusion.21), channel_id=1, source_target_pairs={{0,128},{64,192},{128,0},{192,64},{256,384},{320,448},{384,256},{4... | collective-permute-start | bytes 82952 | tf_op jit(solution)/shard_map/ppermute | solution.py:44
  138.7 8.0 %collective-permute-start.3 = (f32[3,192,12]{1,2,0:T(8,128)S(1)}, f32[3,192,12]{1,2,0:T(8,128)S(1)}, u32[]{:S(2)}, u32[]{:S(2)}) collective-permute-start(f32[3,192,12]{1,2,0:T(8,128)S(1)} %fusion.24), channel_id=1, source_target_pairs={{0,256},{64,320},{128,384},{192,448},{256,0},{320,64},{384,128},{4... | collective-permute-start | bytes 82952 | tf_op jit(solution)/shard_map/ppermute | solution.py:44
  146.7 14.5 %collective-permute-start.4 = (f32[3,192,12]{1,2,0:T(8,128)S(1)}, f32[3,192,12]{1,2,0:T(8,128)S(1)}, u32[]{:S(2)}, u32[]{:S(2)}) collective-permute-start(f32[3,192,12]{1,2,0:T(8,128)S(1)} %add.40), channel_id=1, source_target_pairs={{0,512},{64,576},{128,640},{192,704},{256,768},{320,832},{384,896}... | collective-permute-start | bytes 82952 | tf_op jit(solution)/shard_map/ppermute | solution.py:44

commit v6 on v5

--- a/solution.py
+++ b/solution.py
@@ -32,18 +32,18 @@
     gathered = lax.all_to_all(outgoing, MEM, 0, 0, tiled=True)
     grad = gathered.reshape(dim, hid)
     left = jnp.dot(g_inverse[0], grad, preferred_element_type=jnp.float32).astype(jnp.bfloat16)
-    term = jnp.dot(left, a_inverse[0], preferred_element_type=jnp.float32)
-    pieces = jnp.transpose(term.reshape(dim, members, width), (1, 0, 2))
+    flipped = jnp.einsum("ek,kh->he", left, a_inverse[0], preferred_element_type=jnp.float32)
+    pieces = flipped.reshape(members, width, dim)
     returned = lax.all_to_all(pieces, MEM, 0, 0, tiled=True)
     mine = jnp.stack([returned[owner[0, layer]] for layer in range(layers)])
     groups = lax.axis_size("grp")
     total = mine
-    step = 1
-    while step < groups:
+    step = groups // 2
+    while step >= 1:
         pairs = [(i, i ^ step) for i in range(groups)]
         total = total + lax.ppermute(total, "grp", pairs)
-        step *= 2
-    return total.astype(jnp.bfloat16)
+        step //= 2
+    return jnp.transpose(total, (0, 2, 1)).astype(jnp.bfloat16)
 
 
 def solution(mesh):

time: 163 us -> 161 us (0.988)
  blocking collectives: 0 us -> 26.2 us
  waiting for transfers between devices: 83.7 us -> 65.7 us
  starting transfers between devices: 54.5 us -> 48 us
  local copies, waits for them, and re-layouts: 10.4 us -> 7.48 us
    all_to_all x0 -> x1, blocking collectives: none -> 26.2 us  [shards(): gathered = lax.all_to_all(outgoing, MEM, 0, 0, tiled=True)]
    all_to_all x1 -> x0, waiting for transfers between devices: 14.5 us -> none  [shards(): gathered = lax.all_to_all(outgoing, MEM, 0, 0, tiled=True)]
    all_to_all x1 -> x0, starting transfers between devices: 9.03 us -> none  [shards(): gathered = lax.all_to_all(outgoing, MEM, 0, 0, tiled=True)]
    ppermute x4, waiting for transfers between devices: 12.8 us -> 9.57 us  [shards(): total = total + lax.ppermute(total, 'grp', pairs)]
    ppermute x4, starting transfers between devices: 21.6 us -> 24.2 us  [shards(): total = total + lax.ppermute(total, 'grp', pairs)]
  transfers between devices with their start and end apart: 8 -> 7, of which waited for: 8 -> 7; matrix products, arithmetic and copies ran while one was open for 3% -> 2% of each run, Pallas kernels for 0% -> 0%
where the time goes in v6:
time: 161 us; the launch traced here: 160 us
  waiting for transfers between devices  65.7 us (41%)
  starting transfers between devices  48 us (30%)
  blocking collectives  26.2 us (16%)
  local copies, waits for them, and re-layouts  7.48 us (5%)
  between operations  5.69 us (4%)
  matrix products  3.69 us (2%)
  other arithmetic  3.67 us (2%)
    all_to_all x1, waiting for transfers between devices, shards(): parts = lax.all_to_all(pair, CHIPS, 0, 0, tiled=True)  28.5 us
    all_to_all x1, blocking collectives, shards(): gathered = lax.all_to_all(outgoing, MEM, 0, 0, tiled=True)  26.2 us
    all_to_all x1, waiting for transfers between devices, shards(): returned = lax.all_to_all(pieces, MEM, 0, 0, tiled=True)  25.3 us
    ppermute x4, starting transfers between devices, shards(): total = total + lax.ppermute(total, 'grp', pairs)  24.2 us
    all_to_all x1, starting transfers between devices, shards(): parts = lax.all_to_all(pair, CHIPS, 0, 0, tiled=True)  16.8 us
    ppermute x4, waiting for transfers between devices, shards(): total = total + lax.ppermute(total, 'grp', pairs)  9.57 us
    all_to_all x1, starting transfers between devices, shards(): returned = lax.all_to_all(pieces, MEM, 0, 0, tiled=True)  5.08 us
  transfers between devices with their start and end apart: 7, of which 7 were waited for; matrix products, arithmetic and copies ran while one was open for 2% of the time, Pallas kernels for 0%

profile of v6, /device:TPU:4, one launch (start us, length us, event | category | flops | bytes accessed | tf_op | source)
XLA Modules:
  0.0 160.5 jit_solution(2985688610763138889)
XLA Ops:
  0.0 1.5 reshape.24
  2.3 1.9 %collective-permute-start = (f32[32,3,3,768]{3,0,2,1:T(8,128)S(1)}, f32[32,3,3,768]{3,0,2,1:T(8,128)S(1)}, u32[]{:S(2)}, u32[]{:S(2)}) collective-permute-start(f32[32,3,3,768]{3,0,2,1:T(8,128)S(1)} %fusion.7), channel_id=1, source_target_pairs={{0,1},{1,0},{2,3},{3,2},{4,5},{5,4},{6,7},{7,6},{8,9},{9,8},{10,11... | collective-permute-start | bytes 2654216 | tf_op jit(solution)/shard_map/ppermute | solution.py:25
  4.3 2.4 %collective-permute-done = f32[32,3,3,768]{3,0,2,1:T(8,128)S(1)} collective-permute-done((f32[32,3,3,768]{3,0,2,1:T(8,128)S(1)}, f32[32,3,3,768]{3,0,2,1:T(8,128)S(1)}, u32[]{:S(2)}, u32[]{:S(2)}) %collective-permute-start) | collective-permute-done | bytes 884768 | tf_op jit(solution)/shard_map/ppermute | solution.py:25
  7.2 1.6 %copy.14 = f32[32,3,3,768]{3,2,1,0:T(4,128)} copy(f32[32,3,3,768]{3,0,2,1:T(8,128)S(1)} %fusion.10) | data formatting | bytes 1769472 | tf_op jit(solution)/shard_map/add | solution.py:25
  8.8 16.8 %all-to-all-start = ((f32[32,3,3,768]{3,2,1,0:T(4,128)}), f32[32,3,3,768]{3,2,1,0:T(4,128)S(1)}, u32[]{:S(2)}, u32[]{:S(2)}) async-start(f32[32,3,3,768]{3,2,1,0:T(4,128)} %copy.14), calls=%async_computation | async-start | bytes 2359296 | tf_op jit(solution)/shard_map/all_to_all | solution.py:26
  26.3 0.7 iota_compare_fusion.2
  27.0 1.2 iota_compare_fusion
  28.1 28.5 %all-to-all-done = f32[32,3,3,768]{3,2,1,0:T(4,128)S(1)} async-done(((f32[32,3,3,768]{3,2,1,0:T(4,128)}), f32[32,3,3,768]{3,2,1,0:T(4,128)S(1)}, u32[]{:S(2)}, u32[]{:S(2)}) %all-to-all-start) | async-done | bytes 884768 | tf_op jit(solution)/shard_map/all_to_all | solution.py:26
  56.6 0.8 reduce_sum.9
  57.4 0.7 slice_bitcast_fusion.2
  58.5 26.2 %all_to_all.15 = bf16[64,3,768]{2,1,0:T(4,128)(2,1)S(1)} all-to-all(bf16[64,3,768]{2,1,0:T(4,128)(2,1)S(1)} %select_select_fusion), channel_id=1, replica_groups=mesh['grp'=16,'x'=8,'yh'=4,'core'=2] {'x','yh','core'}, dimensions={0} | all-to-all | bytes 589824 | tf_op jit(solution)/shard_map/all_to_all | solution.py:32
  84.9 2.7 %convolution_bitcast_fusion = f32[768,192]{0,1:T(8,128)} fusion(bf16[1,768,768]{2,1,0:T(8,128)(2,1)} %param.8, bf16[192,768]{1,0:T(8,128)(2,1)S(1)} %reshape.25, bf16[1,192,192]{2,1,0:T(8,128)(2,1)} %param.9), kind=kOutput, calls=%fused_computation.7 | convolution fusion | flops 283262976 | bytes 2138112 | tf_op jit(solution)/shard_map/ek,kh->he/dot_general | solution.py:35
  87.6 1.3 copy.15
  89.0 1.1 reshape.26
  90.0 5.1 %all-to-all-start.2 = ((f32[64,12,192]{2,1,0:T(8,128)}), f32[64,12,192]{2,1,0:T(8,128)S(1)}, u32[]{:S(2)}, u32[]{:S(2)}) async-start(f32[64,12,192]{2,1,0:T(8,128)} %reshape.26), calls=%async_computation.2 | async-start | bytes 2097152 | tf_op jit(solution)/shard_map/all_to_all | solution.py:37
  100.7 25.3 %all-to-all-done.2 = f32[64,12,192]{2,1,0:T(8,128)S(1)} async-done(((f32[64,12,192]{2,1,0:T(8,128)}), f32[64,12,192]{2,1,0:T(8,128)S(1)}, u32[]{:S(2)}, u32[]{:S(2)}) %all-to-all-start.2) | async-done | bytes 589856 | tf_op jit(solution)/shard_map/all_to_all | solution.py:37
  126.0 11.3 %collective-permute-start.1 = (f32[3,12,192]{2,1,0:T(8,128)S(1)}, f32[3,12,192]{2,1,0:T(8,128)S(1)}, u32[]{:S(2)}, u32[]{:S(2)}) collective-permute-start(f32[3,12,192]{2,1,0:T(8,128)S(1)} %pad_maximum_fusion), channel_id=1, source_target_pairs={{0,512},{64,576},{128,640},{192,704},{256,768},{320,832},{384,896}... | collective-permute-start | bytes 82952 | tf_op jit(solution)/shard_map/ppermute | solution.py:44
  137.3 2.2 %collective-permute-done.1 = f32[3,12,192]{2,1,0:T(8,128)S(1)} collective-permute-done((f32[3,12,192]{2,1,0:T(8,128)S(1)}, f32[3,12,192]{2,1,0:T(8,128)S(1)}, u32[]{:S(2)}, u32[]{:S(2)}) %collective-permute-start.1) | collective-permute-done | bytes 27680 | tf_op jit(solution)/shard_map/ppermute | solution.py:44
  139.4 6.0 %collective-permute-start.2 = (f32[3,12,192]{2,1,0:T(8,128)S(1)}, f32[3,12,192]{2,1,0:T(8,128)S(1)}, u32[]{:S(2)}, u32[]{:S(2)}) collective-permute-start(f32[3,12,192]{2,1,0:T(8,128)S(1)} %fusion.21), channel_id=1, source_target_pairs={{0,256},{64,320},{128,384},{192,448},{256,0},{320,64},{384,128},{4... | collective-permute-start | bytes 82952 | tf_op jit(solution)/shard_map/ppermute | solution.py:44
  145.5 2.1 %collective-permute-done.2 = f32[3,12,192]{2,1,0:T(8,128)S(1)} collective-permute-done((f32[3,12,192]{2,1,0:T(8,128)S(1)}, f32[3,12,192]{2,1,0:T(8,128)S(1)}, u32[]{:S(2)}, u32[]{:S(2)}) %collective-permute-start.2) | collective-permute-done | bytes 27680 | tf_op jit(solution)/shard_map/ppermute | solution.py:44
  147.6 4.2 %collective-permute-start.3 = (f32[3,12,192]{2,1,0:T(8,128)S(1)}, f32[3,12,192]{2,1,0:T(8,128)S(1)}, u32[]{:S(2)}, u32[]{:S(2)}) collective-permute-start(f32[3,12,192]{2,1,0:T(8,128)S(1)} %fusion.24), channel_id=1, source_target_pairs={{0,128},{64,192},{128,0},{192,64},{256,384},{320,448},{384,256},{4... | collective-permute-start | bytes 82952 | tf_op jit(solution)/shard_map/ppermute | solution.py:44
  151.8 2.1 %collective-permute-done.3 = f32[3,12,192]{2,1,0:T(8,128)S(1)} collective-permute-done((f32[3,12,192]{2,1,0:T(8,128)S(1)}, f32[3,12,192]{2,1,0:T(8,128)S(1)}, u32[]{:S(2)}, u32[]{:S(2)}) %collective-permute-start.3) | collective-permute-done | bytes 27680 | tf_op jit(solution)/shard_map/ppermute | solution.py:44
  153.9 2.7 %collective-permute-start.4 = (f32[3,12,192]{2,1,0:T(8,128)S(1)}, f32[3,12,192]{2,1,0:T(8,128)S(1)}, u32[]{:S(2)}, u32[]{:S(2)}) collective-permute-start(f32[3,12,192]{2,1,0:T(8,128)S(1)} %add.40), channel_id=1, source_target_pairs={{0,64},{64,0},{128,192},{192,128},{256,320},{320,256},{384,448},{4... | collective-permute-start | bytes 82952 | tf_op jit(solution)/shard_map/ppermute | solution.py:44
  156.5 3.3 %collective-permute-done.4 = f32[3,12,192]{2,1,0:T(8,128)S(1)} collective-permute-done((f32[3,12,192]{2,1,0:T(8,128)S(1)}, f32[3,12,192]{2,1,0:T(8,128)S(1)}, u32[]{:S(2)}, u32[]{:S(2)}) %collective-permute-start.4) | collective-permute-done | bytes 27680 | tf_op jit(solution)/shard_map/ppermute | solution.py:44
  (16 shorter events, 3.3 us)
Async XLA Ops:
  0.0 1.8 %copy-start = (bf16[3,512,768]{2,1,0:T(8,128)(2,1)S(1)}, bf16[3,512,768]{2,1,0:T(8,128)(2,1)}, u32[]{:S(2)}) copy-start(bf16[3,512,768]{2,1,0:T(8,128)(2,1)} %param.5) | copy-start | bytes 7077892
  2.3 4.3 %collective-permute-start = (f32[32,3,3,768]{3,0,2,1:T(8,128)S(1)}, f32[32,3,3,768]{3,0,2,1:T(8,128)S(1)}, u32[]{:S(2)}, u32[]{:S(2)}) collective-permute-start(f32[32,3,3,768]{3,0,2,1:T(8,128)S(1)} %fusion.7), channel_id=1, source_target_pairs={{0,1},{1,0},{2,3},{3,2},{4,5},{5,4},{6,7},{7,6},{8,9},{9,8},{10,11... | collective-permute-start | bytes 2654216 | tf_op jit(solution)/shard_map/ppermute | solution.py:25
  7.2 18.5 %copy-start.1 = (s32[1,3]{1,0:T(1,128)S(1)}, s32[1,3]{1,0:T(1,128)}, u32[]{:S(2)}) copy-start(s32[1,3]{1,0:T(1,128)} %param.7) | copy-start | bytes 40
  8.8 47.8 %all-to-all-start = ((f32[32,3,3,768]{3,2,1,0:T(4,128)}), f32[32,3,3,768]{3,2,1,0:T(4,128)S(1)}, u32[]{:S(2)}, u32[]{:S(2)}) async-start(f32[32,3,3,768]{3,2,1,0:T(4,128)} %copy.14), calls=%async_computation | async-start | bytes 2359296 | tf_op jit(solution)/shard_map/all_to_all | solution.py:26
  90.0 36.0 %all-to-all-start.2 = ((f32[64,12,192]{2,1,0:T(8,128)}), f32[64,12,192]{2,1,0:T(8,128)S(1)}, u32[]{:S(2)}, u32[]{:S(2)}) async-start(f32[64,12,192]{2,1,0:T(8,128)} %reshape.26), calls=%async_computation.2 | async-start | bytes 2097152 | tf_op jit(solution)/shard_map/all_to_all | solution.py:37
  126.0 13.4 %collective-permute-start.1 = (f32[3,12,192]{2,1,0:T(8,128)S(1)}, f32[3,12,192]{2,1,0:T(8,128)S(1)}, u32[]{:S(2)}, u32[]{:S(2)}) collective-permute-start(f32[3,12,192]{2,1,0:T(8,128)S(1)} %pad_maximum_fusion), channel_id=1, source_target_pairs={{0,512},{64,576},{128,640},{192,704},{256,768},{320,832},{384,896}... | collective-permute-start | bytes 82952 | tf_op jit(solution)/shard_map/ppermute | solution.py:44
  139.4 8.1 %collective-permute-start.2 = (f32[3,12,192]{2,1,0:T(8,128)S(1)}, f32[3,12,192]{2,1,0:T(8,128)S(1)}, u32[]{:S(2)}, u32[]{:S(2)}) collective-permute-start(f32[3,12,192]{2,1,0:T(8,128)S(1)} %fusion.21), channel_id=1, source_target_pairs={{0,256},{64,320},{128,384},{192,448},{256,0},{320,64},{384,128},{4... | collective-permute-start | bytes 82952 | tf_op jit(solution)/shard_map/ppermute | solution.py:44
  147.6 6.3 %collective-permute-start.3 = (f32[3,12,192]{2,1,0:T(8,128)S(1)}, f32[3,12,192]{2,1,0:T(8,128)S(1)}, u32[]{:S(2)}, u32[]{:S(2)}) collective-permute-start(f32[3,12,192]{2,1,0:T(8,128)S(1)} %fusion.24), channel_id=1, source_target_pairs={{0,128},{64,192},{128,0},{192,64},{256,384},{320,448},{384,256},{4... | collective-permute-start | bytes 82952 | tf_op jit(solution)/shard_map/ppermute | solution.py:44
  153.9 6.0 %collective-permute-start.4 = (f32[3,12,192]{2,1,0:T(8,128)S(1)}, f32[3,12,192]{2,1,0:T(8,128)S(1)}, u32[]{:S(2)}, u32[]{:S(2)}) collective-permute-start(f32[3,12,192]{2,1,0:T(8,128)S(1)} %add.40), channel_id=1, source_target_pairs={{0,64},{64,0},{128,192},{192,128},{256,320},{320,256},{384,448},{4... | collective-permute-start | bytes 82952 | tf_op jit(solution)/shard_map/ppermute | solution.py:44

commit v7 on v6

--- a/solution.py
+++ b/solution.py
@@ -25,10 +25,10 @@
     pair = keep + lax.ppermute(send, "core", [(0, 1), (1, 0)])
     parts = lax.all_to_all(pair, CHIPS, 0, 0, tiled=True)
     shard = jnp.sum(parts, axis=0).astype(jnp.bfloat16)
-    slots = lax.broadcasted_iota(jnp.int32, (members, 1, 1), 0)
-    outgoing = jnp.zeros((members, height, hid), jnp.bfloat16)
-    for layer in range(layers):
-        outgoing = jnp.where(slots == owner[0, layer], shard[layer][None], outgoing)
+    slots = lax.broadcasted_iota(jnp.int32, (members, layers), 0)
+    route = (slots == owner[0][None, :]).astype(jnp.bfloat16)
+    outgoing = jnp.einsum("jl,lkh->jkh", route, shard, preferred_element_type=jnp.float32)
+    outgoing = outgoing.astype(jnp.bfloat16)
     gathered = lax.all_to_all(outgoing, MEM, 0, 0, tiled=True)
     grad = gathered.reshape(dim, hid)
     left = jnp.dot(g_inverse[0], grad, preferred_element_type=jnp.float32).astype(jnp.bfloat16)

time: 161 us -> 159 us (0.988)
  blocking collectives: 26.2 us -> 72.9 us
  waiting for transfers between devices: 65.7 us -> 36.6 us
  starting transfers between devices: 48 us -> 31.6 us
  other arithmetic: 3.67 us -> 1.44 us
    all_to_all x0 -> x1, blocking collectives: none -> 50.3 us  [shards(): parts = lax.all_to_all(pair, CHIPS, 0, 0, tiled=True)]
    all_to_all x1 -> x0, waiting for transfers between devices: 28.5 us -> none  [shards(): parts = lax.all_to_all(pair, CHIPS, 0, 0, tiled=True)]
    all_to_all x1 -> x0, starting transfers between devices: 16.8 us -> none  [shards(): parts = lax.all_to_all(pair, CHIPS, 0, 0, tiled=True)]
    all_to_all x1, blocking collectives: 26.2 us -> 22.6 us  [shards(): gathered = lax.all_to_all(outgoing, MEM, 0, 0, tiled=True)]
    eq x2 -> x0, other arithmetic: 1.86 us -> none  [shards(): outgoing = jnp.where(slots == owner[0, layer], shard[layer][None], outgoing)]
  transfers between devices with their start and end apart: 7 -> 6, of which waited for: 7 -> 6; matrix products, arithmetic and copies ran while one was open for 2% -> 0% of each run, Pallas kernels for 0% -> 0%
where the time goes in v7:
time: 159 us
  blocking collectives  72.9 us (46%)
  waiting for transfers between devices  36.6 us (23%)
  starting transfers between devices  31.6 us (20%)
  local copies, waits for them, and re-layouts  5.95 us (4%)
  between operations  5.68 us (4%)
  matrix products  4.73 us (3%)
    all_to_all x1, blocking collectives, shards(): parts = lax.all_to_all(pair, CHIPS, 0, 0, tiled=True)  50.3 us
    all_to_all x1, waiting for transfers between devices, shards(): returned = lax.all_to_all(pieces, MEM, 0, 0, tiled=True)  24.7 us
    ppermute x4, starting transfers between devices, shards(): total = total + lax.ppermute(total, 'grp', pairs)  24.6 us
    all_to_all x1, blocking collectives, shards(): gathered = lax.all_to_all(outgoing, MEM, 0, 0, tiled=True)  22.6 us
    ppermute x4, waiting for transfers between devices, shards(): total = total + lax.ppermute(total, 'grp', pairs)  9.46 us
    all_to_all x1, starting transfers between devices, shards(): returned = lax.all_to_all(pieces, MEM, 0, 0, tiled=True)  5.07 us
  transfers between devices with their start and end apart: 6, of which 6 were waited for; matrix products, arithmetic and copies ran while one was open for 0% of the time, Pallas kernels for 0%

profile of v7, /device:TPU:4, one launch (start us, length us, event | category | flops | bytes accessed | tf_op | source)
XLA Modules:
  0.0 158.9 jit_solution(14238330827163820186)
XLA Ops:
  0.0 1.5 reshape.9
  2.3 1.9 %collective-permute-start = (f32[32,3,3,768]{3,0,2,1:T(8,128)S(1)}, f32[32,3,3,768]{3,0,2,1:T(8,128)S(1)}, u32[]{:S(2)}, u32[]{:S(2)}) collective-permute-start(f32[32,3,3,768]{3,0,2,1:T(8,128)S(1)} %fusion.7), channel_id=1, source_target_pairs={{0,1},{1,0},{2,3},{3,2},{4,5},{5,4},{6,7},{7,6},{8,9},{9,8},{10,11... | collective-permute-start | bytes 2654216 | tf_op jit(solution)/shard_map/ppermute | solution.py:25
  4.3 2.4 %collective-permute-done = f32[32,3,3,768]{3,0,2,1:T(8,128)S(1)} collective-permute-done((f32[32,3,3,768]{3,0,2,1:T(8,128)S(1)}, f32[32,3,3,768]{3,0,2,1:T(8,128)S(1)}, u32[]{:S(2)}, u32[]{:S(2)}) %collective-permute-start) | collective-permute-done | bytes 884768 | tf_op jit(solution)/shard_map/ppermute | solution.py:25
  6.7 0.5 fusion.10
  7.2 0.6 copy.16
  7.8 50.3 %all_to_all.15 = f32[32,3,3,768]{3,2,1,0:T(4,128)S(1)} all-to-all(f32[32,3,3,768]{3,2,1,0:T(4,128)S(1)} %copy.16), channel_id=1, replica_groups=mesh['grp'=16,'x'=8,'yh'=4,'core'=2] {'x','yh'}, dimensions={0} | all-to-all | bytes 1769472 | tf_op jit(solution)/shard_map/all_to_all | solution.py:26
  58.1 0.8 reduce_sum.9
  58.9 1.1 convolution_convert_fusion.1
  60.2 22.6 %all_to_all.16 = bf16[64,3,768]{2,1,0:T(4,128)(2,1)S(1)} all-to-all(bf16[64,3,768]{2,1,0:T(4,128)(2,1)S(1)} %copy.18), channel_id=1, replica_groups=mesh['grp'=16,'x'=8,'yh'=4,'core'=2] {'x','yh','core'}, dimensions={0} | all-to-all | bytes 589824 | tf_op jit(solution)/shard_map/all_to_all | solution.py:32
  83.1 2.6 %convolution_bitcast_fusion = f32[768,192]{0,1:T(8,128)} fusion(bf16[1,768,768]{2,1,0:T(8,128)(2,1)} %param.8, bf16[192,768]{1,0:T(8,128)(2,1)S(1)} %reshape.10, bf16[1,192,192]{2,1,0:T(8,128)(2,1)S(1)} %copy-done.1), kind=kOutput, calls=%fused_computation.7 | convolution fusion | flops 283262976 | bytes 2138112 | tf_op jit(solution)/shard_map/ek,kh->he/dot_general | solution.py:35
  85.8 1.3 copy.19
  87.1 1.1 reshape.11
  88.2 5.1 %all-to-all-start.2 = ((f32[64,12,192]{2,1,0:T(8,128)}), f32[64,12,192]{2,1,0:T(8,128)S(1)}, u32[]{:S(2)}, u32[]{:S(2)}) async-start(f32[64,12,192]{2,1,0:T(8,128)} %reshape.11), calls=%async_computation.2 | async-start | bytes 2097152 | tf_op jit(solution)/shard_map/all_to_all | solution.py:37
  93.2 0.6 fusion.26
  99.4 24.7 %all-to-all-done.2 = f32[64,12,192]{2,1,0:T(8,128)S(1)} async-done(((f32[64,12,192]{2,1,0:T(8,128)}), f32[64,12,192]{2,1,0:T(8,128)S(1)}, u32[]{:S(2)}, u32[]{:S(2)}) %all-to-all-start.2) | async-done | bytes 589856 | tf_op jit(solution)/shard_map/all_to_all | solution.py:37
  124.1 11.5 %collective-permute-start.1 = (f32[3,12,192]{2,1,0:T(8,128)S(1)}, f32[3,12,192]{2,1,0:T(8,128)S(1)}, u32[]{:S(2)}, u32[]{:S(2)}) collective-permute-start(f32[3,12,192]{2,1,0:T(8,128)S(1)} %pad_maximum_fusion), channel_id=1, source_target_pairs={{0,512},{64,576},{128,640},{192,704},{256,768},{320,832},{384,896}... | collective-permute-start | bytes 82952 | tf_op jit(solution)/shard_map/ppermute | solution.py:44
  135.6 2.2 %collective-permute-done.1 = f32[3,12,192]{2,1,0:T(8,128)S(1)} collective-permute-done((f32[3,12,192]{2,1,0:T(8,128)S(1)}, f32[3,12,192]{2,1,0:T(8,128)S(1)}, u32[]{:S(2)}, u32[]{:S(2)}) %collective-permute-start.1) | collective-permute-done | bytes 27680 | tf_op jit(solution)/shard_map/ppermute | solution.py:44
  137.8 6.1 %collective-permute-start.2 = (f32[3,12,192]{2,1,0:T(8,128)S(1)}, f32[3,12,192]{2,1,0:T(8,128)S(1)}, u32[]{:S(2)}, u32[]{:S(2)}) collective-permute-start(f32[3,12,192]{2,1,0:T(8,128)S(1)} %fusion.25), channel_id=1, source_target_pairs={{0,256},{64,320},{128,384},{192,448},{256,0},{320,64},{384,128},{4... | collective-permute-start | bytes 82952 | tf_op jit(solution)/shard_map/ppermute | solution.py:44
  143.9 2.1 %collective-permute-done.2 = f32[3,12,192]{2,1,0:T(8,128)S(1)} collective-permute-done((f32[3,12,192]{2,1,0:T(8,128)S(1)}, f32[3,12,192]{2,1,0:T(8,128)S(1)}, u32[]{:S(2)}, u32[]{:S(2)}) %collective-permute-start.2) | collective-permute-done | bytes 27680 | tf_op jit(solution)/shard_map/ppermute | solution.py:44
  146.0 4.2 %collective-permute-start.3 = (f32[3,12,192]{2,1,0:T(8,128)S(1)}, f32[3,12,192]{2,1,0:T(8,128)S(1)}, u32[]{:S(2)}, u32[]{:S(2)}) collective-permute-start(f32[3,12,192]{2,1,0:T(8,128)S(1)} %fusion.28), channel_id=1, source_target_pairs={{0,128},{64,192},{128,0},{192,64},{256,384},{320,448},{384,256},{4... | collective-permute-start | bytes 82952 | tf_op jit(solution)/shard_map/ppermute | solution.py:44
  150.2 2.1 %collective-permute-done.3 = f32[3,12,192]{2,1,0:T(8,128)S(1)} collective-permute-done((f32[3,12,192]{2,1,0:T(8,128)S(1)}, f32[3,12,192]{2,1,0:T(8,128)S(1)}, u32[]{:S(2)}, u32[]{:S(2)}) %collective-permute-start.3) | collective-permute-done | bytes 27680 | tf_op jit(solution)/shard_map/ppermute | solution.py:44
  152.3 2.8 %collective-permute-start.4 = (f32[3,12,192]{2,1,0:T(8,128)S(1)}, f32[3,12,192]{2,1,0:T(8,128)S(1)}, u32[]{:S(2)}, u32[]{:S(2)}) collective-permute-start(f32[3,12,192]{2,1,0:T(8,128)S(1)} %add.40), channel_id=1, source_target_pairs={{0,64},{64,0},{128,192},{192,128},{256,320},{320,256},{384,448},{4... | collective-permute-start | bytes 82952 | tf_op jit(solution)/shard_map/ppermute | solution.py:44
  155.0 3.2 %collective-permute-done.4 = f32[3,12,192]{2,1,0:T(8,128)S(1)} collective-permute-done((f32[3,12,192]{2,1,0:T(8,128)S(1)}, f32[3,12,192]{2,1,0:T(8,128)S(1)}, u32[]{:S(2)}, u32[]{:S(2)}) %collective-permute-start.4) | collective-permute-done | bytes 27680 | tf_op jit(solution)/shard_map/ppermute | solution.py:44
  158.2 0.6 fusion.20
  (15 shorter events, 1.4 us)
Async XLA Ops:
  0.0 1.8 %copy-start = (bf16[3,512,768]{2,1,0:T(8,128)(2,1)S(1)}, bf16[3,512,768]{2,1,0:T(8,128)(2,1)}, u32[]{:S(2)}) copy-start(bf16[3,512,768]{2,1,0:T(8,128)(2,1)} %param.5) | copy-start | bytes 7077892
  2.3 4.3 %collective-permute-start = (f32[32,3,3,768]{3,0,2,1:T(8,128)S(1)}, f32[32,3,3,768]{3,0,2,1:T(8,128)S(1)}, u32[]{:S(2)}, u32[]{:S(2)}) collective-permute-start(f32[32,3,3,768]{3,0,2,1:T(8,128)S(1)} %fusion.7), channel_id=1, source_target_pairs={{0,1},{1,0},{2,3},{3,2},{4,5},{5,4},{6,7},{7,6},{8,9},{9,8},{10,11... | collective-permute-start | bytes 2654216 | tf_op jit(solution)/shard_map/ppermute | solution.py:25
  7.2 51.7 %copy-start.2 = (s32[1,3]{1,0:T(1,128)S(1)}, s32[1,3]{1,0:T(1,128)}, u32[]{:S(2)}) copy-start(s32[1,3]{1,0:T(1,128)} %param.7) | copy-start | bytes 40
  58.9 24.3 %copy-start.1 = (bf16[1,192,192]{2,1,0:T(8,128)(2,1)S(1)}, bf16[1,192,192]{2,1,0:T(8,128)(2,1)}, u32[]{:S(2)}) copy-start(bf16[1,192,192]{2,1,0:T(8,128)(2,1)} %param.9) | copy-start | bytes 221188
  88.2 35.9 %all-to-all-start.2 = ((f32[64,12,192]{2,1,0:T(8,128)}), f32[64,12,192]{2,1,0:T(8,128)S(1)}, u32[]{:S(2)}, u32[]{:S(2)}) async-start(f32[64,12,192]{2,1,0:T(8,128)} %reshape.11), calls=%async_computation.2 | async-start | bytes 2097152 | tf_op jit(solution)/shard_map/all_to_all | solution.py:37
  124.1 13.7 %collective-permute-start.1 = (f32[3,12,192]{2,1,0:T(8,128)S(1)}, f32[3,12,192]{2,1,0:T(8,128)S(1)}, u32[]{:S(2)}, u32[]{:S(2)}) collective-permute-start(f32[3,12,192]{2,1,0:T(8,128)S(1)} %pad_maximum_fusion), channel_id=1, source_target_pairs={{0,512},{64,576},{128,640},{192,704},{256,768},{320,832},{384,896}... | collective-permute-start | bytes 82952 | tf_op jit(solution)/shard_map/ppermute | solution.py:44
  137.8 8.2 %collective-permute-start.2 = (f32[3,12,192]{2,1,0:T(8,128)S(1)}, f32[3,12,192]{2,1,0:T(8,128)S(1)}, u32[]{:S(2)}, u32[]{:S(2)}) collective-permute-start(f32[3,12,192]{2,1,0:T(8,128)S(1)} %fusion.25), channel_id=1, source_target_pairs={{0,256},{64,320},{128,384},{192,448},{256,0},{320,64},{384,128},{4... | collective-permute-start | bytes 82952 | tf_op jit(solution)/shard_map/ppermute | solution.py:44
  146.0 6.3 %collective-permute-start.3 = (f32[3,12,192]{2,1,0:T(8,128)S(1)}, f32[3,12,192]{2,1,0:T(8,128)S(1)}, u32[]{:S(2)}, u32[]{:S(2)}) collective-permute-start(f32[3,12,192]{2,1,0:T(8,128)S(1)} %fusion.28), channel_id=1, source_target_pairs={{0,128},{64,192},{128,0},{192,64},{256,384},{320,448},{384,256},{4... | collective-permute-start | bytes 82952 | tf_op jit(solution)/shard_map/ppermute | solution.py:44
  152.3 6.0 %collective-permute-start.4 = (f32[3,12,192]{2,1,0:T(8,128)S(1)}, f32[3,12,192]{2,1,0:T(8,128)S(1)}, u32[]{:S(2)}, u32[]{:S(2)}) collective-permute-start(f32[3,12,192]{2,1,0:T(8,128)S(1)} %add.40), channel_id=1, source_target_pairs={{0,64},{64,0},{128,192},{192,128},{256,320},{320,256},{384,448},{4... | collective-permute-start | bytes 82952 | tf_op jit(solution)/shard_map/ppermute | solution.py:44

commit v8 on v7

--- a/solution.py
+++ b/solution.py
@@ -20,11 +20,11 @@
     blocks = cot.reshape(layers, rows, members // cores, cores, height)
     mine_rows = lax.dynamic_index_in_dim(blocks, core, 3, keepdims=False)
     other_rows = lax.dynamic_index_in_dim(blocks, 1 - core, 3, keepdims=False)
-    keep = jnp.einsum("lrmk,lrh->mlkh", mine_rows, act, preferred_element_type=jnp.float32)
-    send = jnp.einsum("lrmk,lrh->mlkh", other_rows, act, preferred_element_type=jnp.float32)
+    keep = jnp.einsum("lrmk,lrh->mklh", mine_rows, act, preferred_element_type=jnp.float32)
+    send = jnp.einsum("lrmk,lrh->mklh", other_rows, act, preferred_element_type=jnp.float32)
     pair = keep + lax.ppermute(send, "core", [(0, 1), (1, 0)])
     parts = lax.all_to_all(pair, CHIPS, 0, 0, tiled=True)
-    shard = jnp.sum(parts, axis=0).astype(jnp.bfloat16)
+    shard = jnp.transpose(jnp.sum(parts, axis=0), (1, 0, 2)).astype(jnp.bfloat16)
     slots = lax.broadcasted_iota(jnp.int32, (members, layers), 0)
     route = (slots == owner[0][None, :]).astype(jnp.bfloat16)
     outgoing = jnp.einsum("jl,lkh->jkh", route, shard, preferred_element_type=jnp.float32)

time: 159 us -> 160 us (level)
  no operation moved by 1% of the time
where the time goes in v8:
time: 160 us; the launch traced here: 159 us
  blocking collectives  72.9 us (46%)
  waiting for transfers between devices  36.6 us (23%)
  starting transfers between devices  31.6 us (20%)
  local copies, waits for them, and re-layouts  6.03 us (4%)
  between operations  5.68 us (4%)
  matrix products  4.73 us (3%)
    all_to_all x1, blocking collectives, shards(): parts = lax.all_to_all(pair, CHIPS, 0, 0, tiled=True)  50.3 us
    all_to_all x1, waiting for transfers between devices, shards(): returned = lax.all_to_all(pieces, MEM, 0, 0, tiled=True)  24.7 us
    ppermute x4, starting transfers between devices, shards(): total = total + lax.ppermute(total, 'grp', pairs)  24.6 us
    all_to_all x1, blocking collectives, shards(): gathered = lax.all_to_all(outgoing, MEM, 0, 0, tiled=True)  22.6 us
    ppermute x4, waiting for transfers between devices, shards(): total = total + lax.ppermute(total, 'grp', pairs)  9.48 us
    all_to_all x1, starting transfers between devices, shards(): returned = lax.all_to_all(pieces, MEM, 0, 0, tiled=True)  5.08 us
  transfers between devices with their start and end apart: 6, of which 6 were waited for; matrix products, arithmetic and copies ran while one was open for 0% of the time, Pallas kernels for 0%

profile of v8, /device:TPU:4, one launch (start us, length us, event | category | flops | bytes accessed | tf_op | source)
XLA Modules:
  0.0 159.0 jit_solution(17295254804607214369)
XLA Ops:
  0.0 1.5 reshape.9
  2.4 1.9 %collective-permute-start = (f32[32,3,3,768]{3,0,2,1:T(8,128)S(1)}, f32[32,3,3,768]{3,0,2,1:T(8,128)S(1)}, u32[]{:S(2)}, u32[]{:S(2)}) collective-permute-start(f32[32,3,3,768]{3,0,2,1:T(8,128)S(1)} %copy.18), channel_id=1, source_target_pairs={{0,1},{1,0},{2,3},{3,2},{4,5},{5,4},{6,7},{7,6},{8,9},{9,8},{10,11... | collective-permute-start | bytes 2654216 | tf_op jit(solution)/shard_map/ppermute | solution.py:25
  4.4 2.4 %collective-permute-done = f32[32,3,3,768]{3,0,2,1:T(8,128)S(1)} collective-permute-done((f32[32,3,3,768]{3,0,2,1:T(8,128)S(1)}, f32[32,3,3,768]{3,0,2,1:T(8,128)S(1)}, u32[]{:S(2)}, u32[]{:S(2)}) %collective-permute-start) | collective-permute-done | bytes 884768 | tf_op jit(solution)/shard_map/ppermute | solution.py:25
  6.7 0.5 copy_add_fusion
  7.3 0.6 copy.20
  7.9 50.3 %all_to_all.15 = f32[32,3,3,768]{3,1,2,0:T(4,128)S(1)} all-to-all(f32[32,3,3,768]{3,1,2,0:T(4,128)S(1)} %copy.20), channel_id=1, replica_groups=mesh['grp'=16,'x'=8,'yh'=4,'core'=2] {'x','yh'}, dimensions={0} | all-to-all | bytes 1769472 | tf_op jit(solution)/shard_map/all_to_all | solution.py:26
  58.1 0.8 reduce_sum.9
  58.9 1.1 convolution_convert_fusion.1
  60.3 22.6 %all_to_all.16 = bf16[64,3,768]{2,1,0:T(4,128)(2,1)S(1)} all-to-all(bf16[64,3,768]{2,1,0:T(4,128)(2,1)S(1)} %copy.22), channel_id=1, replica_groups=mesh['grp'=16,'x'=8,'yh'=4,'core'=2] {'x','yh','core'}, dimensions={0} | all-to-all | bytes 589824 | tf_op jit(solution)/shard_map/all_to_all | solution.py:32
  83.2 2.6 %convolution_bitcast_fusion = f32[768,192]{0,1:T(8,128)} fusion(bf16[1,768,768]{2,1,0:T(8,128)(2,1)} %param.8, bf16[192,768]{1,0:T(8,128)(2,1)S(1)} %reshape.10, bf16[1,192,192]{2,1,0:T(8,128)(2,1)S(1)} %copy-done.1), kind=kOutput, calls=%fused_computation.6 | convolution fusion | flops 283262976 | bytes 2138112 | tf_op jit(solution)/shard_map/ek,kh->he/dot_general | solution.py:35
  85.8 1.3 copy.23
  87.2 1.1 reshape.11
  88.2 5.1 %all-to-all-start.2 = ((f32[64,12,192]{2,1,0:T(8,128)}), f32[64,12,192]{2,1,0:T(8,128)S(1)}, u32[]{:S(2)}, u32[]{:S(2)}) async-start(f32[64,12,192]{2,1,0:T(8,128)} %reshape.11), calls=%async_computation.2 | async-start | bytes 2097152 | tf_op jit(solution)/shard_map/all_to_all | solution.py:37
  93.3 0.6 fusion.27
  99.5 24.7 %all-to-all-done.2 = f32[64,12,192]{2,1,0:T(8,128)S(1)} async-done(((f32[64,12,192]{2,1,0:T(8,128)}), f32[64,12,192]{2,1,0:T(8,128)S(1)}, u32[]{:S(2)}, u32[]{:S(2)}) %all-to-all-start.2) | async-done | bytes 589856 | tf_op jit(solution)/shard_map/all_to_all | solution.py:37
  124.2 11.5 %collective-permute-start.1 = (f32[3,12,192]{2,1,0:T(8,128)S(1)}, f32[3,12,192]{2,1,0:T(8,128)S(1)}, u32[]{:S(2)}, u32[]{:S(2)}) collective-permute-start(f32[3,12,192]{2,1,0:T(8,128)S(1)} %pad_maximum_fusion), channel_id=1, source_target_pairs={{0,512},{64,576},{128,640},{192,704},{256,768},{320,832},{384,896}... | collective-permute-start | bytes 82952 | tf_op jit(solution)/shard_map/ppermute | solution.py:44
  135.7 2.2 %collective-permute-done.1 = f32[3,12,192]{2,1,0:T(8,128)S(1)} collective-permute-done((f32[3,12,192]{2,1,0:T(8,128)S(1)}, f32[3,12,192]{2,1,0:T(8,128)S(1)}, u32[]{:S(2)}, u32[]{:S(2)}) %collective-permute-start.1) | collective-permute-done | bytes 27680 | tf_op jit(solution)/shard_map/ppermute | solution.py:44
  137.9 6.1 %collective-permute-start.2 = (f32[3,12,192]{2,1,0:T(8,128)S(1)}, f32[3,12,192]{2,1,0:T(8,128)S(1)}, u32[]{:S(2)}, u32[]{:S(2)}) collective-permute-start(f32[3,12,192]{2,1,0:T(8,128)S(1)} %fusion.26), channel_id=1, source_target_pairs={{0,256},{64,320},{128,384},{192,448},{256,0},{320,64},{384,128},{4... | collective-permute-start | bytes 82952 | tf_op jit(solution)/shard_map/ppermute | solution.py:44
  144.0 2.1 %collective-permute-done.2 = f32[3,12,192]{2,1,0:T(8,128)S(1)} collective-permute-done((f32[3,12,192]{2,1,0:T(8,128)S(1)}, f32[3,12,192]{2,1,0:T(8,128)S(1)}, u32[]{:S(2)}, u32[]{:S(2)}) %collective-permute-start.2) | collective-permute-done | bytes 27680 | tf_op jit(solution)/shard_map/ppermute | solution.py:44
  146.1 4.2 %collective-permute-start.3 = (f32[3,12,192]{2,1,0:T(8,128)S(1)}, f32[3,12,192]{2,1,0:T(8,128)S(1)}, u32[]{:S(2)}, u32[]{:S(2)}) collective-permute-start(f32[3,12,192]{2,1,0:T(8,128)S(1)} %fusion.29), channel_id=1, source_target_pairs={{0,128},{64,192},{128,0},{192,64},{256,384},{320,448},{384,256},{4... | collective-permute-start | bytes 82952 | tf_op jit(solution)/shard_map/ppermute | solution.py:44
  150.3 2.1 %collective-permute-done.3 = f32[3,12,192]{2,1,0:T(8,128)S(1)} collective-permute-done((f32[3,12,192]{2,1,0:T(8,128)S(1)}, f32[3,12,192]{2,1,0:T(8,128)S(1)}, u32[]{:S(2)}, u32[]{:S(2)}) %collective-permute-start.3) | collective-permute-done | bytes 27680 | tf_op jit(solution)/shard_map/ppermute | solution.py:44
  152.4 2.8 %collective-permute-start.4 = (f32[3,12,192]{2,1,0:T(8,128)S(1)}, f32[3,12,192]{2,1,0:T(8,128)S(1)}, u32[]{:S(2)}, u32[]{:S(2)}) collective-permute-start(f32[3,12,192]{2,1,0:T(8,128)S(1)} %add.40), channel_id=1, source_target_pairs={{0,64},{64,0},{128,192},{192,128},{256,320},{320,256},{384,448},{4... | collective-permute-start | bytes 82952 | tf_op jit(solution)/shard_map/ppermute | solution.py:44
  155.1 3.2 %collective-permute-done.4 = f32[3,12,192]{2,1,0:T(8,128)S(1)} collective-permute-done((f32[3,12,192]{2,1,0:T(8,128)S(1)}, f32[3,12,192]{2,1,0:T(8,128)S(1)}, u32[]{:S(2)}, u32[]{:S(2)}) %collective-permute-start.4) | collective-permute-done | bytes 27680 | tf_op jit(solution)/shard_map/ppermute | solution.py:44
  158.3 0.6 fusion.21
  (16 shorter events, 1.5 us)
Async XLA Ops:
  0.0 1.8 %copy-start = (bf16[3,512,768]{2,1,0:T(8,128)(2,1)S(1)}, bf16[3,512,768]{2,1,0:T(8,128)(2,1)}, u32[]{:S(2)}) copy-start(bf16[3,512,768]{2,1,0:T(8,128)(2,1)} %param.5) | copy-start | bytes 7077892
  2.4 4.3 %collective-permute-start = (f32[32,3,3,768]{3,0,2,1:T(8,128)S(1)}, f32[32,3,3,768]{3,0,2,1:T(8,128)S(1)}, u32[]{:S(2)}, u32[]{:S(2)}) collective-permute-start(f32[32,3,3,768]{3,0,2,1:T(8,128)S(1)} %copy.18), channel_id=1, source_target_pairs={{0,1},{1,0},{2,3},{3,2},{4,5},{5,4},{6,7},{7,6},{8,9},{9,8},{10,11... | collective-permute-start | bytes 2654216 | tf_op jit(solution)/shard_map/ppermute | solution.py:25
  7.3 51.7 %copy-start.2 = (s32[1,3]{1,0:T(1,128)S(1)}, s32[1,3]{1,0:T(1,128)}, u32[]{:S(2)}) copy-start(s32[1,3]{1,0:T(1,128)} %param.7) | copy-start | bytes 40
  58.9 24.3 %copy-start.1 = (bf16[1,192,192]{2,1,0:T(8,128)(2,1)S(1)}, bf16[1,192,192]{2,1,0:T(8,128)(2,1)}, u32[]{:S(2)}) copy-start(bf16[1,192,192]{2,1,0:T(8,128)(2,1)} %param.9) | copy-start | bytes 221188
  88.2 36.0 %all-to-all-start.2 = ((f32[64,12,192]{2,1,0:T(8,128)}), f32[64,12,192]{2,1,0:T(8,128)S(1)}, u32[]{:S(2)}, u32[]{:S(2)}) async-start(f32[64,12,192]{2,1,0:T(8,128)} %reshape.11), calls=%async_computation.2 | async-start | bytes 2097152 | tf_op jit(solution)/shard_map/all_to_all | solution.py:37
  124.2 13.7 %collective-permute-start.1 = (f32[3,12,192]{2,1,0:T(8,128)S(1)}, f32[3,12,192]{2,1,0:T(8,128)S(1)}, u32[]{:S(2)}, u32[]{:S(2)}) collective-permute-start(f32[3,12,192]{2,1,0:T(8,128)S(1)} %pad_maximum_fusion), channel_id=1, source_target_pairs={{0,512},{64,576},{128,640},{192,704},{256,768},{320,832},{384,896}... | collective-permute-start | bytes 82952 | tf_op jit(solution)/shard_map/ppermute | solution.py:44
  137.9 8.1 %collective-permute-start.2 = (f32[3,12,192]{2,1,0:T(8,128)S(1)}, f32[3,12,192]{2,1,0:T(8,128)S(1)}, u32[]{:S(2)}, u32[]{:S(2)}) collective-permute-start(f32[3,12,192]{2,1,0:T(8,128)S(1)} %fusion.26), channel_id=1, source_target_pairs={{0,256},{64,320},{128,384},{192,448},{256,0},{320,64},{384,128},{4... | collective-permute-start | bytes 82952 | tf_op jit(solution)/shard_map/ppermute | solution.py:44
  146.1 6.3 %collective-permute-start.3 = (f32[3,12,192]{2,1,0:T(8,128)S(1)}, f32[3,12,192]{2,1,0:T(8,128)S(1)}, u32[]{:S(2)}, u32[]{:S(2)}) collective-permute-start(f32[3,12,192]{2,1,0:T(8,128)S(1)} %fusion.29), channel_id=1, source_target_pairs={{0,128},{64,192},{128,0},{192,64},{256,384},{320,448},{384,256},{4... | collective-permute-start | bytes 82952 | tf_op jit(solution)/shard_map/ppermute | solution.py:44
  152.4 6.0 %collective-permute-start.4 = (f32[3,12,192]{2,1,0:T(8,128)S(1)}, f32[3,12,192]{2,1,0:T(8,128)S(1)}, u32[]{:S(2)}, u32[]{:S(2)}) collective-permute-start(f32[3,12,192]{2,1,0:T(8,128)S(1)} %add.40), channel_id=1, source_target_pairs={{0,64},{64,0},{128,192},{192,128},{256,320},{320,256},{384,448},{4... | collective-permute-start | bytes 82952 | tf_op jit(solution)/shard_map/ppermute | solution.py:44
